TPU v7x, 256 devices: a whole 4x4x8 slice. The times are simulated.
256 devices in a mesh: dp: 4 (over x), expert: 64 (over z, y, core).
Axes of the slice: x: 4, y: 4, z: 8, core: 2. Of those that a mesh axis runs over, the one named last changes fastest.
Arguments:
- hidden_in: bfloat16 [16384, 2048], P(('dp', 'expert')), may hold values from -6 to 6
- context: bfloat16 [16384, 2, 2048], P(('dp', 'expert')), may hold values from -6 to 6
- att_routes: int32 [16384, 2], P(('dp', 'expert')), may hold values from 0 to 7, all different within a row; in each aligned block of 64 rows (0 to 63, 64 to 127, ...) at most 20 rows name the same one
- att_logits: float32 [16384, 8], P(('dp', 'expert')), may hold values from -6 to 6
- ffn_routes: int32 [16384, 2], P(('dp', 'expert')), may hold values from 0 to 7, all different within a row; in each aligned block of 64 rows (0 to 63, 64 to 127, ...) at most 20 rows name the same one
- ffn_logits: float32 [16384, 8], P(('dp', 'expert')), may hold values from -6 to 6
- att_output_map: bfloat16 [64, 2048, 256], P('expert', 'dp'), may hold values from -0.125 to 0.125
- ffn_gate_up: bfloat16 [64, 2048, 2, 704], P('expert', 'dp'), may hold values from -0.125 to 0.125
- ffn_down: bfloat16 [64, 704, 2048], P('expert', None, 'dp'), may hold values from -0.078125 to 0.078125
- norm_gain: bfloat16 [2048], replicated, may hold values from 0.5 to 1.5
- out_gain: bfloat16 [2048], replicated, may hold values from 0.5 to 1.5
Outputs:
- layer_out: bfloat16 [16384, 2048], P(('dp', 'expert'))
Inputs may be any that keep to these rules, and one draw needn't show every extreme that they name: `att_routes`: the two ids of a row differ. In the rows of one device no attention expert is named more than 20 times, and on some device one is named exactly 20 times. `ffn_routes`: the two ids of a row differ. In the rows of one device no feed-forward expert is named more than 20 times, and on some device one is named exactly 20 times.
All inputs are finite; a program needn't handle non-finite values.
Results may differ from a plain program's by a relative error of at most 0.0054.
Values may be sent and summed in bfloat16 or wider, within the bound.
No kernel may reach another device: no remote copies, remote signals or barrier semaphores. Data moves between devices by JAX's collectives and lax.ppermute only.
A program may use at most 128 MiB of HBM per device.

v0:
```python
import jax
import jax.numpy as jnp
from jax import lax
from jax.sharding import PartitionSpec as P

EXPERTS = 8
CAP = 20


EPSILON = 1e-06


def norm_rows(values, gain):
    mean_square = jnp.mean(values * values, axis=-1, keepdims=True)
    return values * lax.rsqrt(mean_square + EPSILON) * gain.astype(jnp.float32)


def pair_weights(logits, routes):
    expert_ids = jnp.arange(logits.shape[1], dtype=jnp.int32)
    selected = routes[:, :, None] == expert_ids[None, None, :]
    chosen = jnp.sum(jnp.where(selected, logits[:, None, :], 0.0), axis=2)
    first_weight = jax.nn.sigmoid(chosen[:, 0] - chosen[:, 1])
    return jnp.stack([first_weight, 1.0 - first_weight], axis=1)


def slot_matrix(routes, capacity, experts):
    route_list = routes.reshape(-1)
    onehot = (route_list[:, None] == jnp.arange(experts, dtype=jnp.int32)[None, :]).astype(
        jnp.int32
    )
    before = jnp.cumsum(onehot, axis=0) - onehot
    slot_index = jnp.sum(before * onehot, axis=1)
    target = route_list * capacity + slot_index
    slot_ids = jnp.arange(experts * capacity, dtype=jnp.int32)
    return slot_ids[:, None] == target[None, :]


def local(
    hidden_in,
    context,
    att_routes,
    att_logits,
    ffn_routes,
    ffn_logits,
    att_output_map,
    ffn_gate_up,
    ffn_down,
    norm_gain,
    out_gain,
):
    rows_dev = hidden_in.shape[0]
    model_width = hidden_in.shape[1]
    att_dim = context.shape[2]
    out_slice = att_output_map.shape[2]
    hid_slice = ffn_gate_up.shape[3]
    groups = lax.axis_size("expert")
    slices = groups // EXPERTS
    capacity = CAP
    att_weight = pair_weights(att_logits, att_routes)
    att_place = slot_matrix(att_routes, capacity, EXPERTS)
    outgoing = jnp.dot(
        att_place.astype(jnp.bfloat16),
        context.reshape(-1, att_dim),
        preferred_element_type=jnp.float32,
    ).astype(jnp.bfloat16)
    outgoing = jnp.broadcast_to(
        outgoing.reshape(EXPERTS, 1, capacity, att_dim), (EXPERTS, slices, capacity, att_dim)
    ).reshape(groups, capacity, att_dim)
    incoming = lax.all_to_all(outgoing, "expert", split_axis=0, concat_axis=0, tiled=True)
    item_count = incoming.shape[1]
    flattened = incoming.reshape(-1, att_dim)
    columns = flattened
    running = jnp.dot(
        columns,
        lax.all_gather(att_output_map, "dp", axis=1, tiled=True)[0],
        preferred_element_type=jnp.float32,
    )
    mapped = running.astype(jnp.bfloat16).reshape(groups, item_count, out_slice)
    returned = lax.all_to_all(mapped, "expert", split_axis=0, concat_axis=2, tiled=True).reshape(
        capacity, EXPERTS, model_width
    )
    picked = jnp.einsum(
        "ecq,ced->qd",
        att_place.reshape(EXPERTS, capacity, -1).astype(jnp.bfloat16),
        returned,
        preferred_element_type=jnp.float32,
    )
    picked = picked.reshape(rows_dev, 2, model_width)
    hidden_state = (
        hidden_in.astype(jnp.float32)
        + att_weight[:, 0:1] * picked[:, 0]
        + att_weight[:, 1:2] * picked[:, 1]
    )
    ffn_in = norm_rows(hidden_state, norm_gain).astype(jnp.bfloat16)
    ffn_place = slot_matrix(ffn_routes, capacity, EXPERTS)
    row_place = jnp.any(ffn_place.reshape(EXPERTS * capacity, rows_dev, 2), axis=2)
    outgoing_rows = jnp.dot(
        row_place.astype(jnp.bfloat16), ffn_in, preferred_element_type=jnp.float32
    ).astype(jnp.bfloat16)
    outgoing_rows = jnp.broadcast_to(
        outgoing_rows.reshape(EXPERTS, 1, capacity, model_width),
        (EXPERTS, slices, capacity, model_width),
    ).reshape(groups, capacity, model_width)
    incoming = lax.all_to_all(outgoing_rows, "expert", split_axis=0, concat_axis=0, tiled=True)
    item_count = incoming.shape[1]
    flattened = incoming.reshape(-1, model_width)
    shard_piece = lax.all_gather(ffn_gate_up, "dp", axis=1, tiled=True)
    depth = shard_piece.shape[1]
    columns = flattened
    gate_up = jnp.dot(
        columns, shard_piece[0].reshape(depth, 2 * hid_slice), preferred_element_type=jnp.float32
    )
    gate_up = gate_up.reshape(-1, 2, hid_slice)
    activated = (jax.nn.silu(gate_up[:, 0]) * gate_up[:, 1]).astype(jnp.bfloat16)
    hidden_units = activated.reshape(groups, item_count, hid_slice)
    hidden_list = hidden_units.reshape(-1, hid_slice)
    projected = jnp.dot(
        hidden_list,
        lax.all_gather(ffn_down, "dp", axis=2, tiled=True)[0],
        preferred_element_type=jnp.float32,
    ).astype(jnp.bfloat16)
    returned_rows = lax.all_to_all(
        projected.reshape(groups, capacity, model_width),
        "expert",
        split_axis=0,
        concat_axis=0,
        tiled=True,
    )
    summed = jnp.sum(
        returned_rows.reshape(EXPERTS, slices, capacity, model_width).astype(jnp.float32), axis=1
    )
    summed = summed.reshape(EXPERTS * capacity, model_width)
    ffn_weight = pair_weights(ffn_logits, ffn_routes)
    weighted = ffn_place.astype(jnp.float32) * ffn_weight.reshape(1, -1)
    expert_mix = jnp.dot(weighted.T, summed, precision=lax.Precision.HIGHEST).reshape(
        rows_dev, 2, model_width
    )
    mixed_sum = hidden_state + (expert_mix[:, 0] + expert_mix[:, 1])
    return norm_rows(mixed_sum, out_gain).astype(jnp.bfloat16)


def solution(mesh):
    return jax.shard_map(
        local,
        mesh=mesh,
        in_specs=(
            P(("dp", "expert"), None),
            P(("dp", "expert"), None, None),
            P(("dp", "expert"), None),
            P(("dp", "expert"), None),
            P(("dp", "expert"), None),
            P(("dp", "expert"), None),
            P("expert", "dp", None),
            P("expert", "dp", None, None),
            P("expert", None, "dp"),
            P(),
            P(),
        ),
        out_specs=P(("dp", "expert"), None),
        check_vma=False,
    )
```

profile of v0, /device:TPU:1, one launch (start us, length us, event | category | flops | bytes accessed | tf_op | source)
XLA Modules:
  0.0 562.6 jit_solution(6501533463382614022)
XLA Ops:
  6.5 0.8 copy.49
  7.9 1.2 reshape.143
  9.6 3.4 broadcast_in_dim.29
  13.1 13.5 %all-to-all-start = ((bf16[64,20,2048]{2,1,0:T(8,128)(2,1)}), bf16[64,20,2048]{2,1,0:T(8,128)(2,1)}, u32[]{:S(2)}, u32[]{:S(2)}) async-start(bf16[64,20,2048]{2,1,0:T(8,128)(2,1)} %bitcast.67), calls=%async_computation | async-start | bytes 12582912 | tf_op jit(solution)/shard_map/all_to_all | solution.py:69
  26.6 0.7 all-gather.4.cloned.1.call-update
  27.3 0.7 all-gather.6.cloned.1.call-update
  28.5 136.6 %all-to-all-done = bf16[64,20,2048]{2,1,0:T(8,128)(2,1)} async-done(((bf16[64,20,2048]{2,1,0:T(8,128)(2,1)}), bf16[64,20,2048]{2,1,0:T(8,128)(2,1)}, u32[]{:S(2)}, u32[]{:S(2)}) %all-to-all-start) | async-done | bytes 5242912 | tf_op jit(solution)/shard_map/all_to_all | solution.py:69
  165.1 9.0 %reshape.145 = bf16[1280,2048]{1,0:T(8,128)(2,1)} reshape(bf16[64,20,2048]{2,1,0:T(8,128)(2,1)} %all-to-all-done) | data formatting | bytes 10485760 | tf_op jit(solution)/shard_map/reshape | solution.py:71
  174.1 4.3 convolution_convert_fusion.1
  178.4 1.0 reshape.146
  179.4 8.3 %all-to-all-start.1 = ((bf16[64,20,256]{2,1,0:T(8,128)(2,1)}), bf16[64,20,256]{2,1,0:T(8,128)(2,1)S(1)}, u32[]{:S(2)}, u32[]{:S(2)}) async-start(bf16[64,20,256]{2,1,0:T(8,128)(2,1)} %reshape.146), calls=%async_computation.1 | async-start | bytes 1572864 | tf_op jit(solution)/shard_map/all_to_all | solution.py:79
  188.6 21.9 %all-to-all-done.1 = bf16[64,20,256]{2,1,0:T(8,128)(2,1)S(1)} async-done(((bf16[64,20,256]{2,1,0:T(8,128)(2,1)}), bf16[64,20,256]{2,1,0:T(8,128)(2,1)S(1)}, u32[]{:S(2)}, u32[]{:S(2)}) %all-to-all-start.1) | async-done | bytes 655392 | tf_op jit(solution)/shard_map/all_to_all | solution.py:79
  212.4 3.4 broadcast_in_dim.54
  215.9 6.4 %all-to-all-start.2 = ((bf16[64,20,2048]{2,1,0:T(8,128)(2,1)}), bf16[64,20,2048]{2,1,0:T(8,128)(2,1)}, u32[]{:S(2)}, u32[]{:S(2)}) async-start(bf16[64,20,2048]{2,1,0:T(8,128)(2,1)} %bitcast.68), calls=%async_computation.2 | async-start | bytes 12582912 | tf_op jit(solution)/shard_map/all_to_all | solution.py:104
  223.0 137.8 %all-to-all-done.2 = bf16[64,20,2048]{2,1,0:T(8,128)(2,1)} async-done(((bf16[64,20,2048]{2,1,0:T(8,128)(2,1)}), bf16[64,20,2048]{2,1,0:T(8,128)(2,1)}, u32[]{:S(2)}, u32[]{:S(2)}) %all-to-all-start.2) | async-done | bytes 5242912 | tf_op jit(solution)/shard_map/all_to_all | solution.py:104
  360.8 9.0 %reshape.156 = bf16[1280,2048,1]{1,0,2:T(8,128)(2,1)} reshape(bf16[64,20,2048]{2,1,0:T(8,128)(2,1)} %all-to-all-done.2) | data formatting | bytes 10485760 | tf_op jit(solution)/shard_map/reshape | solution.py:106
  369.8 13.1 %fusion = f32[1280,2,704]{0,2,1:T(8,128)} fusion(bf16[1280,2048,1]{1,0,2:T(8,128)(2,1)} %reshape.156, bf16[1,2048,2,704]{1,3,2,0:T(8,128)(2,1)} %all-gather.6.cloned.1.call-done), kind=kOutput, calls=%fused_computation.2 | convolution fusion | flops 7381975040 | bytes 18219008 | tf_op jit(solution)/shard_map/dot_general | solution.py:110
  382.9 10.6 %convolution_convert_fusion = bf16[1280,2048]{1,0:T(8,128)(2,1)} fusion(bf16[1,704,2048]{2,1,0:T(8,128)(2,1)} %all-gather.8.cloned.1.call-done, f32[1280,2,704]{0,2,1:T(8,128)} %fusion), kind=kOutput, calls=%fused_computation.1 | convolution fusion | flops 3699015680 | bytes 15335424 | tf_op jit(solution)/shard_map/dot_general | solution.py:117
  393.5 8.9 %reshape.151 = bf16[64,20,2048]{2,1,0:T(8,128)(2,1)} reshape(bf16[1280,2048]{1,0:T(8,128)(2,1)} %convolution_convert_fusion) | data formatting | bytes 10485760 | tf_op jit(solution)/shard_map/reshape | solution.py:123
  402.4 8.6 %all-to-all-start.3 = ((bf16[64,20,2048]{2,1,0:T(8,128)(2,1)}), bf16[64,20,2048]{2,1,0:T(8,128)(2,1)}, u32[]{:S(2)}, u32[]{:S(2)}) async-start(bf16[64,20,2048]{2,1,0:T(8,128)(2,1)} %reshape.151), calls=%async_computation.3 | async-start | bytes 12582912 | tf_op jit(solution)/shard_map/all_to_all | solution.py:122
  411.1 138.4 %all-to-all-done.3 = bf16[64,20,2048]{2,1,0:T(8,128)(2,1)} async-done(((bf16[64,20,2048]{2,1,0:T(8,128)(2,1)}), bf16[64,20,2048]{2,1,0:T(8,128)(2,1)}, u32[]{:S(2)}, u32[]{:S(2)}) %all-to-all-start.3) | async-done | bytes 5242912 | tf_op jit(solution)/shard_map/all_to_all | solution.py:122
  549.6 4.2 convert_reduce_fusion
  554.0 1.1 fusion.18
  555.3 0.8 multiply_convert_fusion
  (58 shorter events, 5.4 us)
Async XLA Ops:
  13.1 15.2 %copy-start.2 = (s32[64,2]{0,1:T(2,128)S(1)}, s32[64,2]{0,1:T(2,128)}, u32[]{:S(2)}) copy-start(s32[64,2]{0,1:T(2,128)} %param.15) | copy-start | bytes 1540
  13.1 152.0 %all-to-all-start = ((bf16[64,20,2048]{2,1,0:T(8,128)(2,1)}), bf16[64,20,2048]{2,1,0:T(8,128)(2,1)}, u32[]{:S(2)}, u32[]{:S(2)}) async-start(bf16[64,20,2048]{2,1,0:T(8,128)(2,1)} %bitcast.67), calls=%async_computation | async-start | bytes 12582912 | tf_op jit(solution)/shard_map/all_to_all | solution.py:69
  26.5 147.5 %all-gather.4.cloned.1.call-start = ((), (), s32[]{:S(2)}) async-start(), calls=%async_computation.4 | async-start | bytes 1310720 | tf_op jit(solution)/shard_map/all_gather | solution.py:75
  27.3 342.5 %all-gather.6.cloned.1.call-start = ((), (), s32[]{:S(2)}) async-start(), calls=%async_computation.5 | async-start | bytes 7208960 | tf_op jit(solution)/shard_map/all_gather | solution.py:107
  174.0 14.4 %copy-start.1 = (s32[64,2]{0,1:T(2,128)S(1)}, s32[64,2]{0,1:T(2,128)}, u32[]{:S(2)}) copy-start(s32[64,2]{0,1:T(2,128)} %param.13) | copy-start | bytes 1540
  174.0 14.4 %copy-start.5 = (f32[64,8]{0,1:T(8,128)S(1)}, f32[64,8]{0,1:T(8,128)}, u32[]{:S(2)}) copy-start(f32[64,8]{0,1:T(8,128)} %param.14) | copy-start | bytes 6148
  174.0 14.4 %copy-start.3 = (bf16[2048]{0:T(1024)(128)(2,1)S(1)}, bf16[2048]{0:T(1024)(128)(2,1)}, u32[]{:S(2)}) copy-start(bf16[2048]{0:T(1024)(128)(2,1)} %param.20) | copy-start | bytes 12292
  178.4 33.2 %copy-start = (bf16[64,2048]{1,0:T(8,128)(2,1)S(1)}, bf16[64,2048]{1,0:T(8,128)(2,1)}, u32[]{:S(2)}) copy-start(bf16[64,2048]{1,0:T(8,128)(2,1)} %param.11) | copy-start | bytes 786436
  179.4 31.1 %all-to-all-start.1 = ((bf16[64,20,256]{2,1,0:T(8,128)(2,1)}), bf16[64,20,256]{2,1,0:T(8,128)(2,1)S(1)}, u32[]{:S(2)}, u32[]{:S(2)}) async-start(bf16[64,20,256]{2,1,0:T(8,128)(2,1)} %reshape.146), calls=%async_computation.1 | async-start | bytes 1572864 | tf_op jit(solution)/shard_map/all_to_all | solution.py:79
  215.9 145.0 %all-to-all-start.2 = ((bf16[64,20,2048]{2,1,0:T(8,128)(2,1)}), bf16[64,20,2048]{2,1,0:T(8,128)(2,1)}, u32[]{:S(2)}, u32[]{:S(2)}) async-start(bf16[64,20,2048]{2,1,0:T(8,128)(2,1)} %bitcast.68), calls=%async_computation.2 | async-start | bytes 12582912 | tf_op jit(solution)/shard_map/all_to_all | solution.py:104
  222.3 160.6 %all-gather.8.cloned.1.call-start = ((), (), s32[]{:S(2)}) async-start(), calls=%async_computation.6 | async-start | bytes 3604480 | tf_op jit(solution)/shard_map/all_gather | solution.py:119
  402.4 8.6 %copy-start.4 = (bf16[2048]{0:T(1024)(128)(2,1)S(1)}, bf16[2048]{0:T(1024)(128)(2,1)}, u32[]{:S(2)}) copy-start(bf16[2048]{0:T(1024)(128)(2,1)} %param.21) | copy-start | bytes 12292
  402.4 8.6 %copy-start.6 = (f32[64,8]{0,1:T(8,128)S(1)}, f32[64,8]{0,1:T(8,128)}, u32[]{:S(2)}) copy-start(f32[64,8]{0,1:T(8,128)} %param.16) | copy-start | bytes 6148
  402.4 147.1 %all-to-all-start.3 = ((bf16[64,20,2048]{2,1,0:T(8,128)(2,1)}), bf16[64,20,2048]{2,1,0:T(8,128)(2,1)}, u32[]{:S(2)}, u32[]{:S(2)}) async-start(bf16[64,20,2048]{2,1,0:T(8,128)(2,1)} %reshape.151), calls=%async_computation.3 | async-start | bytes 12582912 | tf_op jit(solution)/shard_map/all_to_all | solution.py:122
Sparse Core Ops, SparseCore 0:
  29.2 26.5 all-gather.3
  57.5 65.0 all-gather.5
  225.0 40.7 all-gather.7
where the time goes:
time: 565 us; the launch traced here: 563 us
  waiting for transfers between devices  437 us (77%)
  local copies, waits for them, and re-layouts  38.5 us (7%)
  starting transfers between devices  37.1 us (7%)
  matrix products  30.5 us (5%)
  between operations  13.4 us (2%)
  other arithmetic  6.59 us (1%)
    all_to_all x1, waiting for transfers between devices, local(): lax.all_to_all(projected.reshape(groups, capacity, model_width), 'expert'...  138 us
    all_to_all x1, waiting for transfers between devices, local(): lax.all_to_all(outgoing_rows, 'expert', split_axis=0, concat_axis=0, tile...  138 us
    all_to_all x1, waiting for transfers between devices, local(): lax.all_to_all(outgoing, 'expert', split_axis=0, concat_axis=0, tiled=True)  137 us
    all_to_all x1, waiting for transfers between devices, local(): lax.all_to_all(mapped, 'expert', split_axis=0, concat_axis=2, tiled=True)  21.9 us
    all_to_all x1, starting transfers between devices, local(): lax.all_to_all(outgoing, 'expert', split_axis=0, concat_axis=0, tiled=True)  13.5 us
    dot_general x1, matrix products, local(): jnp.dot(columns, shard_piece[0].reshape(depth, 2 * hid_slice), preferred_...  13.1 us
  transfers between devices with their start and end apart: 7, of which 4 were waited for; matrix products, arithmetic and copies ran while one was open for 8% of the time, Pallas kernels for 0%

commit v1 on v0

v1 whole, which is shorter than its diff:
```python
import jax
import jax.numpy as jnp
import numpy as np
from jax import lax
from jax.sharding import Mesh
from jax.sharding import PartitionSpec as P

EXPERTS = 8
CAP = 20


EPSILON = 1e-06


def norm_rows(values, gain):
    mean_square = jnp.mean(values * values, axis=-1, keepdims=True)
    return values * lax.rsqrt(mean_square + EPSILON) * gain.astype(jnp.float32)


def pair_weights(logits, routes):
    expert_ids = jnp.arange(logits.shape[1], dtype=jnp.int32)
    selected = routes[:, :, None] == expert_ids[None, None, :]
    chosen = jnp.sum(jnp.where(selected, logits[:, None, :], 0.0), axis=2)
    first_weight = jax.nn.sigmoid(chosen[:, 0] - chosen[:, 1])
    return jnp.stack([first_weight, 1.0 - first_weight], axis=1)


def slot_matrix(routes, capacity, experts):
    route_list = routes.reshape(-1)
    onehot = (route_list[:, None] == jnp.arange(experts, dtype=jnp.int32)[None, :]).astype(
        jnp.int32
    )
    before = jnp.cumsum(onehot, axis=0) - onehot
    slot_index = jnp.sum(before * onehot, axis=1)
    target = route_list * capacity + slot_index
    slot_ids = jnp.arange(experts * capacity, dtype=jnp.int32)
    return slot_ids[:, None] == target[None, :]


def dispatch(blocks):
    arrived = lax.all_to_all(blocks, "ez", split_axis=0, concat_axis=0, tiled=True)
    n_eh = lax.axis_size("eh")
    copies = jnp.broadcast_to(arrived[None], (n_eh,) + arrived.shape)
    return lax.all_to_all(copies, "eh", split_axis=0, concat_axis=0, tiled=True)


def local(
    hidden_in,
    context,
    att_routes,
    att_logits,
    ffn_routes,
    ffn_logits,
    att_output_map,
    ffn_gate_up,
    ffn_down,
    norm_gain,
    out_gain,
):
    rows_dev = hidden_in.shape[0]
    model_width = hidden_in.shape[1]
    att_dim = context.shape[2]
    out_slice = att_output_map.shape[2]
    hid_slice = ffn_gate_up.shape[3]
    n_ez = lax.axis_size("ez")
    n_eh = lax.axis_size("eh")
    capacity = CAP

    att_matrix = lax.all_gather(att_output_map, "dp", axis=1, tiled=True)[0]
    gate_matrix = lax.all_gather(ffn_gate_up, "dp", axis=1, tiled=True)[0]
    down_matrix = lax.all_gather(ffn_down, "dp", axis=2, tiled=True)[0]

    att_weight = pair_weights(att_logits, att_routes)
    att_place = slot_matrix(att_routes, capacity, EXPERTS)
    outgoing = jnp.dot(
        att_place.astype(jnp.bfloat16),
        context.reshape(-1, att_dim),
        preferred_element_type=jnp.float32,
    ).astype(jnp.bfloat16)
    incoming = dispatch(outgoing.reshape(EXPERTS, capacity, att_dim))
    mapped = jnp.dot(
        incoming.reshape(-1, att_dim), att_matrix, preferred_element_type=jnp.float32
    ).astype(jnp.bfloat16)
    mapped = mapped.reshape(n_eh, n_ez, capacity, out_slice)
    mapped = jnp.transpose(mapped, (1, 0, 2, 3)).reshape(n_ez * n_eh, capacity, out_slice)
    back = lax.all_to_all(mapped, ("ez", "eh"), split_axis=0, concat_axis=0, tiled=True)
    back = back.reshape(EXPERTS, n_eh, capacity, out_slice)
    back = jnp.transpose(back, (0, 2, 1, 3)).reshape(EXPERTS * capacity, model_width)
    picked = jnp.dot(
        att_place.T.astype(jnp.bfloat16), back, preferred_element_type=jnp.float32
    )
    picked = picked.reshape(rows_dev, 2, model_width)
    hidden_state = (
        hidden_in.astype(jnp.float32)
        + att_weight[:, 0:1] * picked[:, 0]
        + att_weight[:, 1:2] * picked[:, 1]
    )
    ffn_in = norm_rows(hidden_state, norm_gain).astype(jnp.bfloat16)
    ffn_place = slot_matrix(ffn_routes, capacity, EXPERTS)
    row_place = jnp.any(ffn_place.reshape(EXPERTS * capacity, rows_dev, 2), axis=2)
    outgoing_rows = jnp.dot(
        row_place.astype(jnp.bfloat16), ffn_in, preferred_element_type=jnp.float32
    ).astype(jnp.bfloat16)
    incoming = dispatch(outgoing_rows.reshape(EXPERTS, capacity, model_width))
    flattened = incoming.reshape(-1, model_width)
    depth = gate_matrix.shape[0]
    gate_up = jnp.dot(
        flattened, gate_matrix.reshape(depth, 2 * hid_slice), preferred_element_type=jnp.float32
    )
    gate_up = gate_up.reshape(-1, 2, hid_slice)
    activated = (jax.nn.silu(gate_up[:, 0]) * gate_up[:, 1]).astype(jnp.bfloat16)
    projected = jnp.dot(
        activated, down_matrix, preferred_element_type=jnp.float32
    ).astype(jnp.bfloat16)
    projected = projected.reshape(n_eh, n_ez, capacity, model_width)
    reduced = lax.psum_scatter(projected, "eh", scatter_dimension=0, tiled=True)[0]
    summed = lax.all_to_all(reduced, "ez", split_axis=0, concat_axis=0, tiled=True)
    summed = summed.reshape(EXPERTS * capacity, model_width).astype(jnp.float32)
    ffn_weight = pair_weights(ffn_logits, ffn_routes)
    weighted = ffn_place.astype(jnp.float32) * ffn_weight.reshape(1, -1)
    expert_mix = jnp.dot(weighted.T, summed, precision=lax.Precision.HIGHEST).reshape(
        rows_dev, 2, model_width
    )
    mixed_sum = hidden_state + (expert_mix[:, 0] + expert_mix[:, 1])
    return norm_rows(mixed_sum, out_gain).astype(jnp.bfloat16)


def solution(mesh):
    n_dp = mesh.devices.shape[0]
    n_expert = mesh.devices.shape[1]
    grid = Mesh(
        mesh.devices.reshape(n_dp, EXPERTS, n_expert // EXPERTS), ("dp", "ez", "eh")
    )
    rows = ("dp", "ez", "eh")
    owners = ("ez", "eh")
    return jax.shard_map(
        local,
        mesh=grid,
        in_specs=(
            P(rows, None),
            P(rows, None, None),
            P(rows, None),
            P(rows, None),
            P(rows, None),
            P(rows, None),
            P(owners, "dp", None),
            P(owners, "dp", None, None),
            P(owners, None, "dp"),
            P(),
            P(),
        ),
        out_specs=P(rows, None),
        check_vma=False,
    )
```

time: 565 us -> 389 us (0.69)
  waiting for transfers between devices: 437 us -> 204 us
  blocking collectives: 0 us -> 55.6 us
  local copies, waits for them, and re-layouts: 38.5 us -> 56.4 us
  starting transfers between devices: 37.1 us -> 26.2 us
    all_to_all x4, waiting for transfers between devices: 435 us -> 163 us  [the longest x2 118 us: dispatch(): return lax.all_to_all(copies, 'eh', split_axis=0, concat_axis=0, tiled=True)]
    all_to_all x0 -> x2, blocking collectives: none -> 55.6 us  [dispatch(): lax.all_to_all(blocks, 'ez', split_axis=0, concat_axis=0, tiled=True)]
    reduce_scatter x0 -> x1, waiting for transfers between devices: none -> 39.1 us  [local(): lax.psum_scatter(projected, 'eh', scatter_dimension=0, tiled=True)[0]]
    all_to_all x1 -> x4, local copies, waits for them, and re-layouts: 0.14 us -> 18.3 us  [the longest x2 17.6 us: dispatch(): return lax.all_to_all(copies, 'eh', split_axis=0, concat_axis=0, tiled=True)]
    all_to_all x4, starting transfers between devices: 36.8 us -> 25.9 us  [the longest x2 14.2 us: dispatch(): return lax.all_to_all(copies, 'eh', split_axis=0, concat_axis=0, tiled=True)]
    reshape x5 -> x8, local copies, waits for them, and re-layouts: 19.3 us -> 20 us  [the longest x1 9.03 us: local(): incoming.reshape(-1, att_dim)]
  transfers between devices with their start and end apart: 7 -> 8, of which waited for: 4 -> 5; matrix products, arithmetic and copies ran while one was open for 8% -> 16% of each run, Pallas kernels for 0% -> 0%
where the time goes in v1:
time: 389 us; the launch traced here: 388 us
  waiting for transfers between devices  204 us (52%)
  local copies, waits for them, and re-layouts  56.4 us (14%)
  blocking collectives  55.6 us (14%)
  matrix products  29.6 us (8%)
  starting transfers between devices  26.2 us (7%)
  between operations  13.4 us (3%)
    all_to_all x2, waiting for transfers between devices, dispatch(): return lax.all_to_all(copies, 'eh', split_axis=0, concat_axis=0, tiled=True)  118 us
    all_to_all x2, blocking collectives, dispatch(): lax.all_to_all(blocks, 'ez', split_axis=0, concat_axis=0, tiled=True)  55.6 us
    reduce_scatter x1, waiting for transfers between devices, local(): lax.psum_scatter(projected, 'eh', scatter_dimension=0, tiled=True)[0]  39.1 us
    all_to_all x1, waiting for transfers between devices, local(): lax.all_to_all(reduced, 'ez', split_axis=0, concat_axis=0, tiled=True)  23.5 us
    all_to_all x1, waiting for transfers between devices, local(): lax.all_to_all(mapped, ('ez', 'eh'), split_axis=0, concat_axis=0, tiled=T...  21.8 us
    all_to_all x2, local copies, waits for them, and re-layouts, dispatch(): return lax.all_to_all(copies, 'eh', split_axis=0, concat_axis=0, tiled=True)  17.6 us
    all_to_all x2, starting transfers between devices, dispatch(): return lax.all_to_all(copies, 'eh', split_axis=0, concat_axis=0, tiled=True)  14.2 us
    dot_general x1, matrix products, local(): jnp.dot(flattened, gate_matrix.reshape(depth, 2 * hid_slice), preferred_e...  13.1 us
  transfers between devices with their start and end apart: 8, of which 5 were waited for; matrix products, arithmetic and copies ran while one was open for 16% of the time, Pallas kernels for 0%

profile of v1, /device:TPU:1, one launch (start us, length us, event | category | flops | bytes accessed | tf_op | source)
XLA Modules:
  0.0 388.0 jit_solution(14187085837249539604)
XLA Ops:
  7.9 1.2 reshape.149
  9.6 30.4 %all_to_all.30 = bf16[8,20,2048]{2,1,0:T(8,128)(2,1)S(1)} all-to-all(bf16[8,20,2048]{2,1,0:T(8,128)(2,1)S(1)} %reshape.150), channel_id=1, replica_groups=mesh['dp'=4,'ez'=8,'eh'=8] {'ez'}, dimensions={0} | all-to-all | bytes 1310720 | tf_op jit(solution)/shard_map/all_to_all | solution.py:41
  40.4 3.0 broadcast_in_dim.24
  43.4 7.0 %all-to-all-start.1 = ((bf16[8,8,20,2048]{3,1,2,0:T(8,128)(2,1)}), bf16[8,8,20,2048]{3,1,2,0:T(8,128)(2,1)}, u32[]{:S(2)}, u32[]{:S(2)}) async-start(bf16[8,8,20,2048]{3,1,2,0:T(8,128)(2,1)} %broadcast_in_dim.24), calls=%async_computation.1 | async-start | bytes 10485760 | tf_op jit(solution)/shard_map/all_to_all | solution.py:44
  51.9 58.7 %all-to-all-done.1 = bf16[8,8,20,2048]{3,1,2,0:T(8,128)(2,1)} async-done(((bf16[8,8,20,2048]{3,1,2,0:T(8,128)(2,1)}), bf16[8,8,20,2048]{3,1,2,0:T(8,128)(2,1)}, u32[]{:S(2)}, u32[]{:S(2)}) %all-to-all-start.1) | async-done | bytes 5242912 | tf_op jit(solution)/shard_map/all_to_all | solution.py:44
  110.6 8.8 %copy.68 = bf16[8,8,20,2048]{3,2,1,0:T(8,128)(2,1)} copy(bf16[8,8,20,2048]{3,1,2,0:T(8,128)(2,1)} %all-to-all-done.1) | data formatting | bytes 10485760 | tf_op jit(solution)/shard_map/all_to_all | solution.py:44
  119.4 9.0 %reshape.151 = bf16[1280,2048]{1,0:T(8,128)(2,1)} reshape(bf16[8,8,20,2048]{3,2,1,0:T(8,128)(2,1)} %copy.68) | data formatting | bytes 10485760 | tf_op jit(solution)/shard_map/reshape | solution.py:82
  128.4 4.3 %convolution_convert_fusion.1 = bf16[1280,256]{1,0:T(8,128)(2,1)S(1)} fusion(bf16[1280,2048]{1,0:T(8,128)(2,1)} %reshape.151, bf16[1,2048,256]{2,1,0:T(8,128)(2,1)} %all-gather.4.cloned.1.call-done), kind=kOutput, calls=%fused_computation.6 | convolution fusion | flops 1342504960 | bytes 6946816 | tf_op jit(solution)/shard_map/dot_general | solution.py:81
  133.3 1.3 copy.70
  134.6 4.9 %all-to-all-start.2 = ((bf16[64,20,256]{2,1,0:T(8,128)(2,1)}), bf16[64,20,256]{2,1,0:T(8,128)(2,1)S(1)}, u32[]{:S(2)}, u32[]{:S(2)}) async-start(bf16[64,20,256]{2,1,0:T(8,128)(2,1)} %copy.70), calls=%async_computation.2 | async-start | bytes 1572864 | tf_op jit(solution)/shard_map/all_to_all | solution.py:86
  140.8 21.8 %all-to-all-done.2 = bf16[64,20,256]{2,1,0:T(8,128)(2,1)S(1)} async-done(((bf16[64,20,256]{2,1,0:T(8,128)(2,1)}), bf16[64,20,256]{2,1,0:T(8,128)(2,1)S(1)}, u32[]{:S(2)}, u32[]{:S(2)}) %all-to-all-start.2) | async-done | bytes 655392 | tf_op jit(solution)/shard_map/all_to_all | solution.py:86
  164.1 25.2 %all_to_all.31 = bf16[8,20,2048]{2,1,0:T(8,128)(2,1)S(1)} all-to-all(bf16[8,20,2048]{2,1,0:T(8,128)(2,1)S(1)} %reshape.157), channel_id=1, replica_groups=mesh['dp'=4,'ez'=8,'eh'=8] {'ez'}, dimensions={0} | all-to-all | bytes 1310720 | tf_op jit(solution)/shard_map/all_to_all | solution.py:41
  189.7 3.0 broadcast_in_dim.26
  192.6 7.2 %all-to-all-start.4 = ((bf16[8,8,20,2048]{3,1,2,0:T(8,128)(2,1)}), bf16[8,8,20,2048]{3,1,2,0:T(8,128)(2,1)}, u32[]{:S(2)}, u32[]{:S(2)}) async-start(bf16[8,8,20,2048]{3,1,2,0:T(8,128)(2,1)} %broadcast_in_dim.26), calls=%async_computation.4 | async-start | bytes 10485760 | tf_op jit(solution)/shard_map/all_to_all | solution.py:44
  200.8 59.2 %all-to-all-done.4 = bf16[8,8,20,2048]{3,1,2,0:T(8,128)(2,1)} async-done(((bf16[8,8,20,2048]{3,1,2,0:T(8,128)(2,1)}), bf16[8,8,20,2048]{3,1,2,0:T(8,128)(2,1)}, u32[]{:S(2)}, u32[]{:S(2)}) %all-to-all-start.4) | async-done | bytes 5242912 | tf_op jit(solution)/shard_map/all_to_all | solution.py:44
  260.0 8.7 %copy.77 = bf16[8,8,20,2048]{3,2,1,0:T(8,128)(2,1)} copy(bf16[8,8,20,2048]{3,1,2,0:T(8,128)(2,1)} %all-to-all-done.4) | data formatting | bytes 10485760 | tf_op jit(solution)/shard_map/all_to_all | solution.py:44
  268.7 9.0 %reshape.162 = bf16[1280,2048,1]{1,0,2:T(8,128)(2,1)} reshape(bf16[8,8,20,2048]{3,2,1,0:T(8,128)(2,1)} %copy.77) | data formatting | bytes 10485760 | tf_op jit(solution)/shard_map/reshape | solution.py:105
  277.7 13.1 %fusion = f32[1280,2,704]{0,2,1:T(8,128)} fusion(bf16[1280,2048,1]{1,0,2:T(8,128)(2,1)} %reshape.162, bf16[1,2048,2,704]{1,3,2,0:T(8,128)(2,1)} %all-gather.6.cloned.1.call-done), kind=kOutput, calls=%fused_computation.1 | convolution fusion | flops 7381975040 | bytes 18219008 | tf_op jit(solution)/shard_map/dot_general | solution.py:107
  290.8 10.6 %convolution_convert_fusion = bf16[1280,2048]{1,0:T(8,128)(2,1)} fusion(bf16[1,704,2048]{2,1,0:T(8,128)(2,1)} %all-gather.8.cloned.1.call-done, f32[1280,2,704]{0,2,1:T(8,128)} %fusion), kind=kOutput, calls=%fused_computation | convolution fusion | flops 3699015680 | bytes 15335424 | tf_op jit(solution)/shard_map/dot_general | solution.py:112
  301.4 8.9 %reshape.159 = bf16[8,8,20,2048]{3,2,1,0:T(8,128)(2,1)} reshape(bf16[1280,2048]{1,0:T(8,128)(2,1)} %convolution_convert_fusion) | data formatting | bytes 10485760 | tf_op jit(solution)/shard_map/reshape | solution.py:115
  310.3 39.1 %reduce-scatter.2.cloned.1.call-done = bf16[1,8,20,2048]{3,2,1,0:T(8,128)(2,1)} async-done(((bf16[8,8,20,2048]{3,2,1,0:T(8,128)(2,1)}), bf16[1,8,20,2048]{3,2,1,0:T(8,128)(2,1)}) %reduce-scatter.2.cloned.1.call-update) | async-done | bytes 655376 | tf_op jit(solution)/shard_map/reduce_scatter | solution.py:116
  349.4 6.7 %all-to-all-start.5 = ((bf16[8,20,2048]{2,1,0:T(8,128)(2,1)}), bf16[8,20,2048]{2,1,0:T(8,128)(2,1)S(1)}, u32[]{:S(2)}, u32[]{:S(2)}) async-start(bf16[8,20,2048]{2,1,0:T(8,128)(2,1)} %bitcast.65), calls=%async_computation.6 | async-start | bytes 1572864 | tf_op jit(solution)/shard_map/all_to_all | solution.py:117
  356.2 23.5 %all-to-all-done.5 = bf16[8,20,2048]{2,1,0:T(8,128)(2,1)S(1)} async-done(((bf16[8,20,2048]{2,1,0:T(8,128)(2,1)}), bf16[8,20,2048]{2,1,0:T(8,128)(2,1)S(1)}, u32[]{:S(2)}, u32[]{:S(2)}) %all-to-all-start.5) | async-done | bytes 655392 | tf_op jit(solution)/shard_map/all_to_all | solution.py:117
  380.7 0.8 multiply_convert_fusion
  (66 shorter events, 9.2 us)
Async XLA Ops:
  43.4 67.2 %all-to-all-start.1 = ((bf16[8,8,20,2048]{3,1,2,0:T(8,128)(2,1)}), bf16[8,8,20,2048]{3,1,2,0:T(8,128)(2,1)}, u32[]{:S(2)}, u32[]{:S(2)}) async-start(bf16[8,8,20,2048]{3,1,2,0:T(8,128)(2,1)} %broadcast_in_dim.24), calls=%async_computation.1 | async-start | bytes 10485760 | tf_op jit(solution)/shard_map/all_to_all | solution.py:44
  50.4 78.0 %all-gather.4.cloned.1.call-start = ((), (), s32[]{:S(2)}) async-start(), calls=%async_computation.7 | async-start | bytes 1310720 | tf_op jit(solution)/shard_map/all_gather | solution.py:69
  51.1 226.6 %all-gather.6.cloned.1.call-start = ((), (), s32[]{:S(2)}) async-start(), calls=%async_computation.8 | async-start | bytes 7208960 | tf_op jit(solution)/shard_map/all_gather | solution.py:70
  132.7 6.9 %copy-start.1 = (s32[64,2]{0,1:T(2,128)S(1)}, s32[64,2]{0,1:T(2,128)}, u32[]{:S(2)}) copy-start(s32[64,2]{0,1:T(2,128)} %param.15) | copy-start | bytes 1540
  132.8 7.8 %copy-start.2 = (bf16[2048]{0:T(1024)(128)(2,1)S(1)}, bf16[2048]{0:T(1024)(128)(2,1)}, u32[]{:S(2)}) copy-start(bf16[2048]{0:T(1024)(128)(2,1)} %param.20) | copy-start | bytes 12292
  132.8 7.8 %copy-start.4 = (f32[64,8]{0,1:T(8,128)S(1)}, f32[64,8]{0,1:T(8,128)}, u32[]{:S(2)}) copy-start(f32[64,8]{0,1:T(8,128)} %param.14) | copy-start | bytes 6148
  132.8 7.8 %copy-start.6 = (s32[64,2]{0,1:T(2,128)S(1)}, s32[64,2]{0,1:T(2,128)}, u32[]{:S(2)}) copy-start(s32[64,2]{0,1:T(2,128)} %param.13) | copy-start | bytes 1540
  132.8 30.5 %copy-start = (bf16[64,2048]{1,0:T(8,128)(2,1)S(1)}, bf16[64,2048]{1,0:T(8,128)(2,1)}, u32[]{:S(2)}) copy-start(bf16[64,2048]{1,0:T(8,128)(2,1)} %param.11) | copy-start | bytes 786436
  134.6 27.9 %all-to-all-start.2 = ((bf16[64,20,256]{2,1,0:T(8,128)(2,1)}), bf16[64,20,256]{2,1,0:T(8,128)(2,1)S(1)}, u32[]{:S(2)}, u32[]{:S(2)}) async-start(bf16[64,20,256]{2,1,0:T(8,128)(2,1)} %copy.70), calls=%async_computation.2 | async-start | bytes 1572864 | tf_op jit(solution)/shard_map/all_to_all | solution.py:86
  192.6 67.3 %all-to-all-start.4 = ((bf16[8,8,20,2048]{3,1,2,0:T(8,128)(2,1)}), bf16[8,8,20,2048]{3,1,2,0:T(8,128)(2,1)}, u32[]{:S(2)}, u32[]{:S(2)}) async-start(bf16[8,8,20,2048]{3,1,2,0:T(8,128)(2,1)} %broadcast_in_dim.26), calls=%async_computation.4 | async-start | bytes 10485760 | tf_op jit(solution)/shard_map/all_to_all | solution.py:44
  199.8 91.0 %all-gather.8.cloned.1.call-start = ((), (), s32[]{:S(2)}) async-start(), calls=%async_computation.9 | async-start | bytes 3604480 | tf_op jit(solution)/shard_map/all_gather | solution.py:71
  200.5 148.9 %reduce-scatter.2.cloned.1.call-start = ((), (), s32[]{:S(2)}) async-start(), calls=%async_computation.10 | async-start | bytes 7077888 | tf_op jit(solution)/shard_map/reduce_scatter | solution.py:116
  310.3 45.8 %copy-start.3 = (bf16[2048]{0:T(1024)(128)(2,1)S(1)}, bf16[2048]{0:T(1024)(128)(2,1)}, u32[]{:S(2)}) copy-start(bf16[2048]{0:T(1024)(128)(2,1)} %param.21) | copy-start | bytes 12292
  310.3 45.9 %copy-start.5 = (f32[64,8]{0,1:T(8,128)S(1)}, f32[64,8]{0,1:T(8,128)}, u32[]{:S(2)}) copy-start(f32[64,8]{0,1:T(8,128)} %param.16) | copy-start | bytes 6148
  349.4 30.3 %all-to-all-start.5 = ((bf16[8,20,2048]{2,1,0:T(8,128)(2,1)}), bf16[8,20,2048]{2,1,0:T(8,128)(2,1)S(1)}, u32[]{:S(2)}, u32[]{:S(2)}) async-start(bf16[8,20,2048]{2,1,0:T(8,128)(2,1)} %bitcast.65), calls=%async_computation.6 | async-start | bytes 1572864 | tf_op jit(solution)/shard_map/all_to_all | solution.py:117
Sparse Core Ops, SparseCore 0:
  53.0 21.6 all-gather.3
  76.5 65.0 all-gather.5
  202.4 35.8 all-gather.7
  310.5 38.9 reduce-scatter.1

commit v2 on v1

--- a/solution.py
+++ b/solution.py
@@ -1,12 +1,12 @@
 import jax
 import jax.numpy as jnp
-import numpy as np
 from jax import lax
 from jax.sharding import Mesh
 from jax.sharding import PartitionSpec as P
 
 EXPERTS = 8
 CAP = 20
+CORES = 2
 
 
 EPSILON = 1e-06
@@ -32,16 +32,18 @@
     )
     before = jnp.cumsum(onehot, axis=0) - onehot
     slot_index = jnp.sum(before * onehot, axis=1)
-    target = route_list * capacity + slot_index
+    target = slot_index * experts + route_list
     slot_ids = jnp.arange(experts * capacity, dtype=jnp.int32)
     return slot_ids[:, None] == target[None, :]
 
 
 def dispatch(blocks):
-    arrived = lax.all_to_all(blocks, "ez", split_axis=0, concat_axis=0, tiled=True)
-    n_eh = lax.axis_size("eh")
-    copies = jnp.broadcast_to(arrived[None], (n_eh,) + arrived.shape)
-    return lax.all_to_all(copies, "eh", split_axis=0, concat_axis=0, tiled=True)
+    arrived = lax.all_to_all(blocks, "ez", split_axis=1, concat_axis=1, tiled=True)
+    n_ey = lax.axis_size("ey")
+    copies = jnp.broadcast_to(arrived[None], (n_ey,) + arrived.shape)
+    across = lax.all_to_all(copies, "ey", split_axis=0, concat_axis=0, tiled=True)
+    pair = jnp.broadcast_to(across[None], (CORES,) + across.shape)
+    return lax.all_to_all(pair, "ec", split_axis=0, concat_axis=0, tiled=True)
 
 
 def local(
@@ -63,7 +65,7 @@
     out_slice = att_output_map.shape[2]
     hid_slice = ffn_gate_up.shape[3]
     n_ez = lax.axis_size("ez")
-    n_eh = lax.axis_size("eh")
+    n_ey = lax.axis_size("ey")
     capacity = CAP
 
     att_matrix = lax.all_gather(att_output_map, "dp", axis=1, tiled=True)[0]
@@ -77,15 +79,17 @@
         context.reshape(-1, att_dim),
         preferred_element_type=jnp.float32,
     ).astype(jnp.bfloat16)
-    incoming = dispatch(outgoing.reshape(EXPERTS, capacity, att_dim))
+    incoming = dispatch(outgoing.reshape(capacity, EXPERTS, att_dim))
     mapped = jnp.dot(
         incoming.reshape(-1, att_dim), att_matrix, preferred_element_type=jnp.float32
     ).astype(jnp.bfloat16)
-    mapped = mapped.reshape(n_eh, n_ez, capacity, out_slice)
-    mapped = jnp.transpose(mapped, (1, 0, 2, 3)).reshape(n_ez * n_eh, capacity, out_slice)
-    back = lax.all_to_all(mapped, ("ez", "eh"), split_axis=0, concat_axis=0, tiled=True)
-    back = back.reshape(EXPERTS, n_eh, capacity, out_slice)
-    back = jnp.transpose(back, (0, 2, 1, 3)).reshape(EXPERTS * capacity, model_width)
+    mapped = mapped.reshape(CORES, n_ey, capacity, n_ez, out_slice)
+    mapped = jnp.transpose(mapped, (3, 1, 0, 2, 4)).reshape(
+        n_ez * n_ey * CORES, capacity, out_slice
+    )
+    back = lax.all_to_all(mapped, ("ez", "ey", "ec"), split_axis=0, concat_axis=0, tiled=True)
+    back = back.reshape(EXPERTS, n_ey * CORES, capacity, out_slice)
+    back = jnp.transpose(back, (2, 0, 1, 3)).reshape(capacity * EXPERTS, model_width)
     picked = jnp.dot(
         att_place.T.astype(jnp.bfloat16), back, preferred_element_type=jnp.float32
     )
@@ -101,7 +105,7 @@
     outgoing_rows = jnp.dot(
         row_place.astype(jnp.bfloat16), ffn_in, preferred_element_type=jnp.float32
     ).astype(jnp.bfloat16)
-    incoming = dispatch(outgoing_rows.reshape(EXPERTS, capacity, model_width))
+    incoming = dispatch(outgoing_rows.reshape(capacity, EXPERTS, model_width))
     flattened = incoming.reshape(-1, model_width)
     depth = gate_matrix.shape[0]
     gate_up = jnp.dot(
@@ -112,10 +116,11 @@
     projected = jnp.dot(
         activated, down_matrix, preferred_element_type=jnp.float32
     ).astype(jnp.bfloat16)
-    projected = projected.reshape(n_eh, n_ez, capacity, model_width)
-    reduced = lax.psum_scatter(projected, "eh", scatter_dimension=0, tiled=True)[0]
-    summed = lax.all_to_all(reduced, "ez", split_axis=0, concat_axis=0, tiled=True)
-    summed = summed.reshape(EXPERTS * capacity, model_width).astype(jnp.float32)
+    projected = projected.reshape(CORES * n_ey, capacity * n_ez, model_width)
+    reduced = lax.psum_scatter(projected, ("ec", "ey"), scatter_dimension=0, tiled=True)[0]
+    reduced = reduced.reshape(capacity, n_ez, model_width)
+    summed = lax.all_to_all(reduced, "ez", split_axis=1, concat_axis=1, tiled=True)
+    summed = summed.reshape(capacity * EXPERTS, model_width).astype(jnp.float32)
     ffn_weight = pair_weights(ffn_logits, ffn_routes)
     weighted = ffn_place.astype(jnp.float32) * ffn_weight.reshape(1, -1)
     expert_mix = jnp.dot(weighted.T, summed, precision=lax.Precision.HIGHEST).reshape(
@@ -128,11 +133,12 @@
 def solution(mesh):
     n_dp = mesh.devices.shape[0]
     n_expert = mesh.devices.shape[1]
+    n_ey = n_expert // (EXPERTS * CORES)
     grid = Mesh(
-        mesh.devices.reshape(n_dp, EXPERTS, n_expert // EXPERTS), ("dp", "ez", "eh")
+        mesh.devices.reshape(n_dp, EXPERTS, n_ey, CORES), ("dp", "ez", "ey", "ec")
     )
-    rows = ("dp", "ez", "eh")
-    owners = ("ez", "eh")
+    rows = ("dp", "ez", "ey", "ec")
+    owners = ("ez", "ey", "ec")
     return jax.shard_map(
         local,
         mesh=grid,

time: 389 us -> 327 us (0.84)
  waiting for transfers between devices: 204 us -> 133 us
  blocking collectives: 55.6 us -> 108 us
  local copies, waits for them, and re-layouts: 56.4 us -> 14.2 us
    all_to_all x4, waiting for transfers between devices: 163 us -> 72.7 us  [the longest x1 23.5 us: local(): lax.all_to_all(reduced, 'ez', split_axis=1, concat_axis=1, tiled=True)]
    all_to_all x2 -> x4, blocking collectives: 55.6 us -> 108 us  [the longest x2 66.5 us: dispatch(): lax.all_to_all(copies, 'ey', split_axis=0, concat_axis=0, tiled=True)]
    reshape x11 -> x5, local copies, waits for them, and re-layouts: 29.3 us -> 4.05 us  [the longest x1 1.39 us: local(): jnp.transpose(mapped, (3, 1, 0, 2, 4))]
    reduce_scatter x1, waiting for transfers between devices: 39.1 us -> 58.6 us  [local(): lax.psum_scatter(projected, ('ec', 'ey'), scatter_dimension=0, tiled=True)]
    all_to_all x4 -> x3, local copies, waits for them, and re-layouts: 18.3 us -> 0.86 us  [the longest x2 0.73 us: dispatch(): lax.all_to_all(blocks, 'ez', split_axis=1, concat_axis=1, tiled=True)]
  transfers between devices with their start and end apart: 8 -> 8, of which waited for: 5 -> 5; matrix products, arithmetic and copies ran while one was open for 16% -> 10% of each run, Pallas kernels for 0% -> 0%
where the time goes in v2:
time: 327 us
  waiting for transfers between devices  133 us (41%)
  blocking collectives  108 us (33%)
  matrix products  29.9 us (9%)
  starting transfers between devices  25.6 us (8%)
  local copies, waits for them, and re-layouts  14.2 us (4%)
  between operations  13.4 us (4%)
    all_to_all x2, blocking collectives, dispatch(): lax.all_to_all(copies, 'ey', split_axis=0, concat_axis=0, tiled=True)  66.5 us
    reduce_scatter x1, waiting for transfers between devices, local(): lax.psum_scatter(projected, ('ec', 'ey'), scatter_dimension=0, tiled=True)  58.6 us
    all_to_all x1, blocking collectives, dispatch(): lax.all_to_all(blocks, 'ez', split_axis=1, concat_axis=1, tiled=True)  30.4 us
    all_to_all x1, waiting for transfers between devices, local(): lax.all_to_all(reduced, 'ez', split_axis=1, concat_axis=1, tiled=True)  23.5 us
    all_to_all x1, waiting for transfers between devices, dispatch(): lax.all_to_all(blocks, 'ez', split_axis=1, concat_axis=1, tiled=True)  22.8 us
    all_to_all x1, waiting for transfers between devices, local(): lax.all_to_all(mapped, ('ez', 'ey', 'ec'), split_axis=0, concat_axis=0, t...  21.5 us
    dot_general x1, matrix products, local(): jnp.dot(flattened, gate_matrix.reshape(depth, 2 * hid_slice), preferred_e...  13.1 us
    all_to_all x1, blocking collectives, dispatch(): return lax.all_to_all(pair, 'ec', split_axis=0, concat_axis=0, tiled=True)  10.7 us
  transfers between devices with their start and end apart: 8, of which 5 were waited for; matrix products, arithmetic and copies ran while one was open for 10% of the time, Pallas kernels for 0%

profile of v2, /device:TPU:1, one launch (start us, length us, event | category | flops | bytes accessed | tf_op | source)
XLA Modules:
  0.0 326.6 jit_solution(955672026809433783)
XLA Ops:
  8.0 0.8 copy.80
  8.9 1.2 reshape.148
  11.3 30.4 %all_to_all.40 = bf16[20,8,2048]{2,0,1:T(8,128)(2,1)S(1)} all-to-all(bf16[20,8,2048]{2,0,1:T(8,128)(2,1)S(1)} %copy.81), channel_id=1, replica_groups=mesh['dp'=4,'ez'=8,'ey'=4,'ec'=2] {'ez'}, dimensions={1} | all-to-all | bytes 1310720 | tf_op jit(solution)/shard_map/all_to_all | solution.py:41
  42.4 33.0 %all_to_all.41 = bf16[4,20,8,2048]{3,2,1,0:T(8,128)(2,1)S(1)} all-to-all(bf16[4,20,8,2048]{3,2,1,0:T(8,128)(2,1)S(1)} %broadcast_in_dim.28), channel_id=1, replica_groups=mesh['dp'=4,'ez'=8,'ey'=4,'ec'=2] {'ey'}, dimensions={0} | all-to-all | bytes 5242880 | tf_op jit(solution)/shard_map/all_to_all | solution.py:44
  75.4 2.9 broadcast_in_dim.29
  78.3 9.9 %all-to-all-start.2 = ((bf16[2,4,20,8,2048]{4,3,2,1,0:T(8,128)(2,1)}), bf16[2,4,20,8,2048]{4,3,2,1,0:T(8,128)(2,1)}, u32[]{:S(2)}, u32[]{:S(2)}) async-start(bf16[2,4,20,8,2048]{4,3,2,1,0:T(8,128)(2,1)} %broadcast_in_dim.29), calls=%async_computation.2 | async-start | bytes 10485760 | tf_op jit(solution)/shard_map/all_to_all | solution.py:46
  88.2 4.9 %all-to-all-done.2 = bf16[2,4,20,8,2048]{4,3,2,1,0:T(8,128)(2,1)} async-done(((bf16[2,4,20,8,2048]{4,3,2,1,0:T(8,128)(2,1)}), bf16[2,4,20,8,2048]{4,3,2,1,0:T(8,128)(2,1)}, u32[]{:S(2)}, u32[]{:S(2)}) %all-to-all-start.2) | async-done | bytes 5242912 | tf_op jit(solution)/shard_map/all_to_all | solution.py:46
  93.1 4.3 %convolution_convert_fusion.1 = bf16[1280,256]{1,0:T(8,128)(2,1)S(1)} fusion(bf16[1280,2048]{1,0:T(8,128)(2,1)} %bitcast.2, bf16[1,2048,256]{2,1,0:T(8,128)(2,1)} %all-gather.4.cloned.1.call-done), kind=kOutput, calls=%fused_computation.6 | convolution fusion | flops 1342504960 | bytes 6946816 | tf_op jit(solution)/shard_map/dot_general | solution.py:83
  98.2 1.4 copy.93
  99.6 4.8 %all-to-all-start.3 = ((bf16[64,20,256]{2,1,0:T(8,128)(2,1)}), bf16[64,20,256]{2,1,0:T(8,128)(2,1)S(1)}, u32[]{:S(2)}, u32[]{:S(2)}) async-start(bf16[64,20,256]{2,1,0:T(8,128)(2,1)} %bitcast.6), calls=%async_computation.3 | async-start | bytes 1572864 | tf_op jit(solution)/shard_map/all_to_all | solution.py:90
  105.6 21.5 %all-to-all-done.3 = bf16[64,20,256]{2,1,0:T(8,128)(2,1)S(1)} async-done(((bf16[64,20,256]{2,1,0:T(8,128)(2,1)}), bf16[64,20,256]{2,1,0:T(8,128)(2,1)S(1)}, u32[]{:S(2)}, u32[]{:S(2)}) %all-to-all-start.3) | async-done | bytes 655392 | tf_op jit(solution)/shard_map/all_to_all | solution.py:90
  128.6 1.3 copy.89
  129.9 4.0 %all-to-all-start.4 = ((bf16[20,8,2048]{2,0,1:T(8,128)(2,1)}), bf16[20,8,2048]{2,0,1:T(8,128)(2,1)S(1)}, u32[]{:S(2)}, u32[]{:S(2)}) async-start(bf16[20,8,2048]{2,0,1:T(8,128)(2,1)} %copy.89), calls=%async_computation.4 | async-start | bytes 1572864 | tf_op jit(solution)/shard_map/all_to_all | solution.py:41
  134.7 22.8 %all-to-all-done.4 = bf16[20,8,2048]{2,0,1:T(8,128)(2,1)S(1)} async-done(((bf16[20,8,2048]{2,0,1:T(8,128)(2,1)}), bf16[20,8,2048]{2,0,1:T(8,128)(2,1)S(1)}, u32[]{:S(2)}, u32[]{:S(2)}) %all-to-all-start.4) | async-done | bytes 655392 | tf_op jit(solution)/shard_map/all_to_all | solution.py:41
  158.2 33.6 %all_to_all.42 = bf16[4,20,8,2048]{3,2,1,0:T(8,128)(2,1)S(1)} all-to-all(bf16[4,20,8,2048]{3,2,1,0:T(8,128)(2,1)S(1)} %broadcast_in_dim.31), channel_id=1, replica_groups=mesh['dp'=4,'ez'=8,'ey'=4,'ec'=2] {'ey'}, dimensions={0} | all-to-all | bytes 5242880 | tf_op jit(solution)/shard_map/all_to_all | solution.py:44
  192.5 10.7 %all_to_all.43 = bf16[2,4,20,8,2048]{4,3,2,1,0:T(8,128)(2,1)} all-to-all(bf16[2,4,20,8,2048]{4,3,2,1,0:T(8,128)(2,1)S(1)} %broadcast_in_dim.32), channel_id=1, replica_groups=mesh['dp'=4,'ez'=8,'ey'=4,'ec'=2] {'ec'}, dimensions={0} | all-to-all | bytes 10485760 | tf_op jit(solution)/shard_map/all_to_all | solution.py:46
  203.1 13.1 %fusion = f32[1280,2,704]{0,2,1:T(8,128)} fusion(bf16[1280,2048,1]{1,0,2:T(8,128)(2,1)} %bitcast.79, bf16[1,2048,2,704]{1,3,2,0:T(8,128)(2,1)} %all-gather.6.cloned.1.call-done), kind=kOutput, calls=%fused_computation.1 | convolution fusion | flops 7381975040 | bytes 18219008 | tf_op jit(solution)/shard_map/dot_general | solution.py:111
  216.2 10.6 %convolution_convert_fusion = bf16[1280,2048]{1,0:T(8,128)(2,1)} fusion(bf16[1,704,2048]{2,1,0:T(8,128)(2,1)} %all-gather.8.cloned.1.call-done, f32[1280,2,704]{0,2,1:T(8,128)} %fusion), kind=kOutput, calls=%fused_computation | convolution fusion | flops 3699015680 | bytes 15335424 | tf_op jit(solution)/shard_map/dot_general | solution.py:116
  226.8 58.6 %reduce-scatter.2.cloned.1.call-done = bf16[1,160,2048]{2,1,0:T(8,128)(2,1)} async-done(((bf16[8,160,2048]{2,1,0:T(8,128)(2,1)}), bf16[1,160,2048]{2,1,0:T(8,128)(2,1)}) %reduce-scatter.2.cloned.1.call-update) | async-done | bytes 655376 | tf_op jit(solution)/shard_map/reduce_scatter | solution.py:120
  285.4 2.3 copy.91
  287.8 6.8 %all-to-all-start.7 = ((bf16[20,8,2048]{2,0,1:T(8,128)(2,1)}), bf16[20,8,2048]{2,0,1:T(8,128)(2,1)S(1)}, u32[]{:S(2)}, u32[]{:S(2)}) async-start(bf16[20,8,2048]{2,0,1:T(8,128)(2,1)} %copy.91), calls=%async_computation.8 | async-start | bytes 1572864 | tf_op jit(solution)/shard_map/all_to_all | solution.py:122
  294.6 23.5 %all-to-all-done.7 = bf16[20,8,2048]{2,0,1:T(8,128)(2,1)S(1)} async-done(((bf16[20,8,2048]{2,0,1:T(8,128)(2,1)}), bf16[20,8,2048]{2,0,1:T(8,128)(2,1)S(1)}, u32[]{:S(2)}, u32[]{:S(2)}) %all-to-all-start.7) | async-done | bytes 655392 | tf_op jit(solution)/shard_map/all_to_all | solution.py:122
  318.1 0.9 fusion.9
  319.2 0.9 multiply_convert_fusion
  (65 shorter events, 9.1 us)
Async XLA Ops:
  6.5 81.7 %all-gather.4.cloned.1.call-start = ((), (), s32[]{:S(2)}) async-start(), calls=%async_computation.9 | async-start | bytes 1310720 | tf_op jit(solution)/shard_map/all_gather | solution.py:71
  7.3 195.9 %all-gather.6.cloned.1.call-start = ((), (), s32[]{:S(2)}) async-start(), calls=%async_computation.10 | async-start | bytes 7208960 | tf_op jit(solution)/shard_map/all_gather | solution.py:72
  78.3 14.8 %all-to-all-start.2 = ((bf16[2,4,20,8,2048]{4,3,2,1,0:T(8,128)(2,1)}), bf16[2,4,20,8,2048]{4,3,2,1,0:T(8,128)(2,1)}, u32[]{:S(2)}, u32[]{:S(2)}) async-start(bf16[2,4,20,8,2048]{4,3,2,1,0:T(8,128)(2,1)} %broadcast_in_dim.29), calls=%async_computation.2 | async-start | bytes 10485760 | tf_op jit(solution)/shard_map/all_to_all | solution.py:46
  97.4 7.1 %copy-start.1 = (s32[64,2]{0,1:T(2,128)S(1)}, s32[64,2]{0,1:T(2,128)}, u32[]{:S(2)}) copy-start(s32[64,2]{0,1:T(2,128)} %param.15) | copy-start | bytes 1540
  97.4 8.0 %copy-start.2 = (bf16[2048]{0:T(1024)(128)(2,1)S(1)}, bf16[2048]{0:T(1024)(128)(2,1)}, u32[]{:S(2)}) copy-start(bf16[2048]{0:T(1024)(128)(2,1)} %param.20) | copy-start | bytes 12292
  97.5 8.0 %copy-start.4 = (f32[64,8]{0,1:T(8,128)S(1)}, f32[64,8]{0,1:T(8,128)}, u32[]{:S(2)}) copy-start(f32[64,8]{0,1:T(8,128)} %param.14) | copy-start | bytes 6148
  97.5 8.0 %copy-start.6 = (s32[64,2]{0,1:T(2,128)S(1)}, s32[64,2]{0,1:T(2,128)}, u32[]{:S(2)}) copy-start(s32[64,2]{0,1:T(2,128)} %param.13) | copy-start | bytes 1540
  99.6 28.3 %copy-start = (bf16[64,2048]{1,0:T(8,128)(2,1)S(1)}, bf16[64,2048]{1,0:T(8,128)(2,1)}, u32[]{:S(2)}) copy-start(bf16[64,2048]{1,0:T(8,128)(2,1)} %param.11) | copy-start | bytes 786436
  99.6 27.6 %all-to-all-start.3 = ((bf16[64,20,256]{2,1,0:T(8,128)(2,1)}), bf16[64,20,256]{2,1,0:T(8,128)(2,1)S(1)}, u32[]{:S(2)}, u32[]{:S(2)}) async-start(bf16[64,20,256]{2,1,0:T(8,128)(2,1)} %bitcast.6), calls=%async_computation.3 | async-start | bytes 1572864 | tf_op jit(solution)/shard_map/all_to_all | solution.py:90
  129.9 27.5 %all-to-all-start.4 = ((bf16[20,8,2048]{2,0,1:T(8,128)(2,1)}), bf16[20,8,2048]{2,0,1:T(8,128)(2,1)S(1)}, u32[]{:S(2)}, u32[]{:S(2)}) async-start(bf16[20,8,2048]{2,0,1:T(8,128)(2,1)} %copy.89), calls=%async_computation.4 | async-start | bytes 1572864 | tf_op jit(solution)/shard_map/all_to_all | solution.py:41
  133.9 82.3 %all-gather.8.cloned.1.call-start = ((), (), s32[]{:S(2)}) async-start(), calls=%async_computation.11 | async-start | bytes 3604480 | tf_op jit(solution)/shard_map/all_gather | solution.py:73
  134.6 150.8 %reduce-scatter.2.cloned.1.call-start = ((), (), s32[]{:S(2)}) async-start(), calls=%async_computation.12 | async-start | bytes 5898240 | tf_op jit(solution)/shard_map/reduce_scatter | solution.py:120
  226.8 67.7 %copy-start.3 = (bf16[2048]{0:T(1024)(128)(2,1)S(1)}, bf16[2048]{0:T(1024)(128)(2,1)}, u32[]{:S(2)}) copy-start(bf16[2048]{0:T(1024)(128)(2,1)} %param.21) | copy-start | bytes 12292
  226.8 67.7 %copy-start.5 = (f32[64,8]{0,1:T(8,128)S(1)}, f32[64,8]{0,1:T(8,128)}, u32[]{:S(2)}) copy-start(f32[64,8]{0,1:T(8,128)} %param.16) | copy-start | bytes 6148
  287.8 30.3 %all-to-all-start.7 = ((bf16[20,8,2048]{2,0,1:T(8,128)(2,1)}), bf16[20,8,2048]{2,0,1:T(8,128)(2,1)S(1)}, u32[]{:S(2)}, u32[]{:S(2)}) async-start(bf16[20,8,2048]{2,0,1:T(8,128)(2,1)} %copy.91), calls=%async_computation.8 | async-start | bytes 1572864 | tf_op jit(solution)/shard_map/all_to_all | solution.py:122
Sparse Core Ops, SparseCore 0:
  9.2 29.3 all-gather.3
  40.4 65.1 all-gather.5
  136.5 40.9 all-gather.7
  227.0 58.4 reduce-scatter.1

commit v3 on v2

--- a/solution.py
+++ b/solution.py
@@ -116,8 +116,10 @@
     projected = jnp.dot(
         activated, down_matrix, preferred_element_type=jnp.float32
     ).astype(jnp.bfloat16)
-    projected = projected.reshape(CORES * n_ey, capacity * n_ez, model_width)
-    reduced = lax.psum_scatter(projected, ("ec", "ey"), scatter_dimension=0, tiled=True)[0]
+    projected = projected.reshape(CORES, n_ey * capacity * n_ez, model_width)
+    reduced = lax.psum_scatter(projected, "ec", scatter_dimension=0, tiled=True)[0]
+    reduced = reduced.reshape(n_ey, capacity * n_ez, model_width)
+    reduced = lax.psum_scatter(reduced, "ey", scatter_dimension=0, tiled=True)[0]
     reduced = reduced.reshape(capacity, n_ez, model_width)
     summed = lax.all_to_all(reduced, "ez", split_axis=1, concat_axis=1, tiled=True)
     summed = summed.reshape(capacity * EXPERTS, model_width).astype(jnp.float32)

time: 327 us -> 322 us (0.985)
  waiting for transfers between devices: 133 us -> 128 us
    reduce_scatter x1 -> x2, waiting for transfers between devices: 58.6 us -> 53 us  [the longest x1 39.9 us: local(): lax.psum_scatter(reduced, 'ey', scatter_dimension=0, tiled=True)[0]]
  transfers between devices with their start and end apart: 8 -> 9, of which waited for: 5 -> 6; matrix products, arithmetic and copies ran while one was open for 10% -> 10% of each run, Pallas kernels for 0% -> 0%
where the time goes in v3:
time: 322 us; the launch traced here: 321 us
  waiting for transfers between devices  128 us (40%)
  blocking collectives  108 us (34%)
  matrix products  29.9 us (9%)
  starting transfers between devices  25.6 us (8%)
  local copies, waits for them, and re-layouts  14.2 us (4%)
  between operations  13.4 us (4%)
    all_to_all x2, blocking collectives, dispatch(): lax.all_to_all(copies, 'ey', split_axis=0, concat_axis=0, tiled=True)  66.5 us
    reduce_scatter x1, waiting for transfers between devices, local(): lax.psum_scatter(reduced, 'ey', scatter_dimension=0, tiled=True)[0]  39.9 us
    all_to_all x1, blocking collectives, dispatch(): lax.all_to_all(blocks, 'ez', split_axis=1, concat_axis=1, tiled=True)  30.4 us
    all_to_all x1, waiting for transfers between devices, local(): lax.all_to_all(reduced, 'ez', split_axis=1, concat_axis=1, tiled=True)  23.5 us
    all_to_all x1, waiting for transfers between devices, dispatch(): lax.all_to_all(blocks, 'ez', split_axis=1, concat_axis=1, tiled=True)  22.8 us
    all_to_all x1, waiting for transfers between devices, local(): lax.all_to_all(mapped, ('ez', 'ey', 'ec'), split_axis=0, concat_axis=0, t...  21.5 us
    reduce_scatter x1, waiting for transfers between devices, local(): lax.psum_scatter(projected, 'ec', scatter_dimension=0, tiled=True)[0]  13.1 us
    dot_general x1, matrix products, local(): jnp.dot(flattened, gate_matrix.reshape(depth, 2 * hid_slice), preferred_e...  13.1 us
  transfers between devices with their start and end apart: 9, of which 6 were waited for; matrix products, arithmetic and copies ran while one was open for 10% of the time, Pallas kernels for 0%

profile of v3, /device:TPU:1, one launch (start us, length us, event | category | flops | bytes accessed | tf_op | source)
XLA Modules:
  0.0 321.0 jit_solution(12703788127804341432)
XLA Ops:
  8.9 1.2 reshape.148
  11.3 30.4 %all_to_all.40 = bf16[20,8,2048]{2,0,1:T(8,128)(2,1)S(1)} all-to-all(bf16[20,8,2048]{2,0,1:T(8,128)(2,1)S(1)} %copy.81), channel_id=1, replica_groups=mesh['dp'=4,'ez'=8,'ey'=4,'ec'=2] {'ez'}, dimensions={1} | all-to-all | bytes 1310720 | tf_op jit(solution)/shard_map/all_to_all | solution.py:41
  42.4 33.0 %all_to_all.41 = bf16[4,20,8,2048]{3,2,1,0:T(8,128)(2,1)S(1)} all-to-all(bf16[4,20,8,2048]{3,2,1,0:T(8,128)(2,1)S(1)} %broadcast_in_dim.28), channel_id=1, replica_groups=mesh['dp'=4,'ez'=8,'ey'=4,'ec'=2] {'ey'}, dimensions={0} | all-to-all | bytes 5242880 | tf_op jit(solution)/shard_map/all_to_all | solution.py:44
  75.4 2.9 broadcast_in_dim.29
  78.3 9.9 %all-to-all-start.2 = ((bf16[2,4,20,8,2048]{4,3,2,1,0:T(8,128)(2,1)}), bf16[2,4,20,8,2048]{4,3,2,1,0:T(8,128)(2,1)}, u32[]{:S(2)}, u32[]{:S(2)}) async-start(bf16[2,4,20,8,2048]{4,3,2,1,0:T(8,128)(2,1)} %broadcast_in_dim.29), calls=%async_computation.2 | async-start | bytes 10485760 | tf_op jit(solution)/shard_map/all_to_all | solution.py:46
  88.2 4.9 %all-to-all-done.2 = bf16[2,4,20,8,2048]{4,3,2,1,0:T(8,128)(2,1)} async-done(((bf16[2,4,20,8,2048]{4,3,2,1,0:T(8,128)(2,1)}), bf16[2,4,20,8,2048]{4,3,2,1,0:T(8,128)(2,1)}, u32[]{:S(2)}, u32[]{:S(2)}) %all-to-all-start.2) | async-done | bytes 5242912 | tf_op jit(solution)/shard_map/all_to_all | solution.py:46
  93.1 4.3 %convolution_convert_fusion.1 = bf16[1280,256]{1,0:T(8,128)(2,1)S(1)} fusion(bf16[1280,2048]{1,0:T(8,128)(2,1)} %bitcast.2, bf16[1,2048,256]{2,1,0:T(8,128)(2,1)} %all-gather.4.cloned.1.call-done), kind=kOutput, calls=%fused_computation.6 | convolution fusion | flops 1342504960 | bytes 6946816 | tf_op jit(solution)/shard_map/dot_general | solution.py:83
  98.2 1.4 copy.93
  99.6 4.8 %all-to-all-start.3 = ((bf16[64,20,256]{2,1,0:T(8,128)(2,1)}), bf16[64,20,256]{2,1,0:T(8,128)(2,1)S(1)}, u32[]{:S(2)}, u32[]{:S(2)}) async-start(bf16[64,20,256]{2,1,0:T(8,128)(2,1)} %bitcast.6), calls=%async_computation.3 | async-start | bytes 1572864 | tf_op jit(solution)/shard_map/all_to_all | solution.py:90
  105.6 21.5 %all-to-all-done.3 = bf16[64,20,256]{2,1,0:T(8,128)(2,1)S(1)} async-done(((bf16[64,20,256]{2,1,0:T(8,128)(2,1)}), bf16[64,20,256]{2,1,0:T(8,128)(2,1)S(1)}, u32[]{:S(2)}, u32[]{:S(2)}) %all-to-all-start.3) | async-done | bytes 655392 | tf_op jit(solution)/shard_map/all_to_all | solution.py:90
  128.6 1.3 copy.89
  129.9 4.0 %all-to-all-start.4 = ((bf16[20,8,2048]{2,0,1:T(8,128)(2,1)}), bf16[20,8,2048]{2,0,1:T(8,128)(2,1)S(1)}, u32[]{:S(2)}, u32[]{:S(2)}) async-start(bf16[20,8,2048]{2,0,1:T(8,128)(2,1)} %copy.89), calls=%async_computation.4 | async-start | bytes 1572864 | tf_op jit(solution)/shard_map/all_to_all | solution.py:41
  134.7 22.8 %all-to-all-done.4 = bf16[20,8,2048]{2,0,1:T(8,128)(2,1)S(1)} async-done(((bf16[20,8,2048]{2,0,1:T(8,128)(2,1)}), bf16[20,8,2048]{2,0,1:T(8,128)(2,1)S(1)}, u32[]{:S(2)}, u32[]{:S(2)}) %all-to-all-start.4) | async-done | bytes 655392 | tf_op jit(solution)/shard_map/all_to_all | solution.py:41
  158.2 33.5 %all_to_all.42 = bf16[4,20,8,2048]{3,2,1,0:T(8,128)(2,1)S(1)} all-to-all(bf16[4,20,8,2048]{3,2,1,0:T(8,128)(2,1)S(1)} %broadcast_in_dim.31), channel_id=1, replica_groups=mesh['dp'=4,'ez'=8,'ey'=4,'ec'=2] {'ey'}, dimensions={0} | all-to-all | bytes 5242880 | tf_op jit(solution)/shard_map/all_to_all | solution.py:44
  192.4 10.7 %all_to_all.43 = bf16[2,4,20,8,2048]{4,3,2,1,0:T(8,128)(2,1)} all-to-all(bf16[2,4,20,8,2048]{4,3,2,1,0:T(8,128)(2,1)S(1)} %broadcast_in_dim.32), channel_id=1, replica_groups=mesh['dp'=4,'ez'=8,'ey'=4,'ec'=2] {'ec'}, dimensions={0} | all-to-all | bytes 10485760 | tf_op jit(solution)/shard_map/all_to_all | solution.py:46
  203.1 13.1 %fusion = f32[1280,2,704]{0,2,1:T(8,128)} fusion(bf16[1280,2048,1]{1,0,2:T(8,128)(2,1)} %bitcast.80, bf16[1,2048,2,704]{1,3,2,0:T(8,128)(2,1)} %all-gather.6.cloned.1.call-done), kind=kOutput, calls=%fused_computation.1 | convolution fusion | flops 7381975040 | bytes 18219008 | tf_op jit(solution)/shard_map/dot_general | solution.py:111
  216.2 10.6 %convolution_convert_fusion = bf16[1280,2048]{1,0:T(8,128)(2,1)} fusion(bf16[1,704,2048]{2,1,0:T(8,128)(2,1)} %all-gather.8.cloned.1.call-done, f32[1280,2,704]{0,2,1:T(8,128)} %fusion), kind=kOutput, calls=%fused_computation | convolution fusion | flops 3699015680 | bytes 15335424 | tf_op jit(solution)/shard_map/dot_general | solution.py:116
  226.9 13.1 %reduce-scatter.3.cloned.1.call-done = bf16[1,640,2048]{2,1,0:T(8,128)(2,1)} async-done(((bf16[2,640,2048]{2,1,0:T(8,128)(2,1)}), bf16[1,640,2048]{2,1,0:T(8,128)(2,1)}) %reduce-scatter.3.cloned.1.call-update) | async-done | bytes 2621456 | tf_op jit(solution)/shard_map/reduce_scatter | solution.py:120
  240.0 39.9 %reduce-scatter.5.cloned.1.call-done = bf16[1,160,2048]{2,1,0:T(8,128)(2,1)} async-done(((bf16[4,160,2048]{2,1,0:T(8,128)(2,1)}), bf16[1,160,2048]{2,1,0:T(8,128)(2,1)}) %reduce-scatter.5.cloned.1.call-update) | async-done | bytes 655376 | tf_op jit(solution)/shard_map/reduce_scatter | solution.py:122
  279.9 2.3 copy.91
  282.2 6.7 %all-to-all-start.7 = ((bf16[20,8,2048]{2,0,1:T(8,128)(2,1)}), bf16[20,8,2048]{2,0,1:T(8,128)(2,1)S(1)}, u32[]{:S(2)}, u32[]{:S(2)}) async-start(bf16[20,8,2048]{2,0,1:T(8,128)(2,1)} %copy.91), calls=%async_computation.9 | async-start | bytes 1572864 | tf_op jit(solution)/shard_map/all_to_all | solution.py:124
  289.0 23.5 %all-to-all-done.7 = bf16[20,8,2048]{2,0,1:T(8,128)(2,1)S(1)} async-done(((bf16[20,8,2048]{2,0,1:T(8,128)(2,1)}), bf16[20,8,2048]{2,0,1:T(8,128)(2,1)S(1)}, u32[]{:S(2)}, u32[]{:S(2)}) %all-to-all-start.7) | async-done | bytes 655392 | tf_op jit(solution)/shard_map/all_to_all | solution.py:124
  312.5 0.9 fusion.9
  313.6 0.8 multiply_convert_fusion
  (68 shorter events, 9.9 us)
Async XLA Ops:
  6.5 81.7 %all-gather.4.cloned.1.call-start = ((), (), s32[]{:S(2)}) async-start(), calls=%async_computation.10 | async-start | bytes 1310720 | tf_op jit(solution)/shard_map/all_gather | solution.py:71
  7.3 195.9 %all-gather.6.cloned.1.call-start = ((), (), s32[]{:S(2)}) async-start(), calls=%async_computation.11 | async-start | bytes 7208960 | tf_op jit(solution)/shard_map/all_gather | solution.py:72
  78.3 14.8 %all-to-all-start.2 = ((bf16[2,4,20,8,2048]{4,3,2,1,0:T(8,128)(2,1)}), bf16[2,4,20,8,2048]{4,3,2,1,0:T(8,128)(2,1)}, u32[]{:S(2)}, u32[]{:S(2)}) async-start(bf16[2,4,20,8,2048]{4,3,2,1,0:T(8,128)(2,1)} %broadcast_in_dim.29), calls=%async_computation.2 | async-start | bytes 10485760 | tf_op jit(solution)/shard_map/all_to_all | solution.py:46
  97.4 7.1 %copy-start.1 = (s32[64,2]{0,1:T(2,128)S(1)}, s32[64,2]{0,1:T(2,128)}, u32[]{:S(2)}) copy-start(s32[64,2]{0,1:T(2,128)} %param.15) | copy-start | bytes 1540
  97.4 8.0 %copy-start.2 = (bf16[2048]{0:T(1024)(128)(2,1)S(1)}, bf16[2048]{0:T(1024)(128)(2,1)}, u32[]{:S(2)}) copy-start(bf16[2048]{0:T(1024)(128)(2,1)} %param.20) | copy-start | bytes 12292
  97.5 8.0 %copy-start.4 = (f32[64,8]{0,1:T(8,128)S(1)}, f32[64,8]{0,1:T(8,128)}, u32[]{:S(2)}) copy-start(f32[64,8]{0,1:T(8,128)} %param.14) | copy-start | bytes 6148
  97.5 8.0 %copy-start.6 = (s32[64,2]{0,1:T(2,128)S(1)}, s32[64,2]{0,1:T(2,128)}, u32[]{:S(2)}) copy-start(s32[64,2]{0,1:T(2,128)} %param.13) | copy-start | bytes 1540
  99.6 28.3 %copy-start = (bf16[64,2048]{1,0:T(8,128)(2,1)S(1)}, bf16[64,2048]{1,0:T(8,128)(2,1)}, u32[]{:S(2)}) copy-start(bf16[64,2048]{1,0:T(8,128)(2,1)} %param.11) | copy-start | bytes 786436
  99.6 27.6 %all-to-all-start.3 = ((bf16[64,20,256]{2,1,0:T(8,128)(2,1)}), bf16[64,20,256]{2,1,0:T(8,128)(2,1)S(1)}, u32[]{:S(2)}, u32[]{:S(2)}) async-start(bf16[64,20,256]{2,1,0:T(8,128)(2,1)} %bitcast.6), calls=%async_computation.3 | async-start | bytes 1572864 | tf_op jit(solution)/shard_map/all_to_all | solution.py:90
  129.9 27.5 %all-to-all-start.4 = ((bf16[20,8,2048]{2,0,1:T(8,128)(2,1)}), bf16[20,8,2048]{2,0,1:T(8,128)(2,1)S(1)}, u32[]{:S(2)}, u32[]{:S(2)}) async-start(bf16[20,8,2048]{2,0,1:T(8,128)(2,1)} %copy.89), calls=%async_computation.4 | async-start | bytes 1572864 | tf_op jit(solution)/shard_map/all_to_all | solution.py:41
  133.9 82.3 %all-gather.8.cloned.1.call-start = ((), (), s32[]{:S(2)}) async-start(), calls=%async_computation.12 | async-start | bytes 3604480 | tf_op jit(solution)/shard_map/all_gather | solution.py:73
  134.6 105.3 %reduce-scatter.3.cloned.1.call-start = ((), (), s32[]{:S(2)}) async-start(), calls=%async_computation.13 | async-start | bytes 7864320 | tf_op jit(solution)/shard_map/reduce_scatter | solution.py:120
  226.8 62.1 %copy-start.3 = (bf16[2048]{0:T(1024)(128)(2,1)S(1)}, bf16[2048]{0:T(1024)(128)(2,1)}, u32[]{:S(2)}) copy-start(bf16[2048]{0:T(1024)(128)(2,1)} %param.21) | copy-start | bytes 12292
  226.8 62.1 %copy-start.5 = (f32[64,8]{0,1:T(8,128)S(1)}, f32[64,8]{0,1:T(8,128)}, u32[]{:S(2)}) copy-start(f32[64,8]{0,1:T(8,128)} %param.16) | copy-start | bytes 6148
  226.8 53.0 %reduce-scatter.5.cloned.1.call-start = ((), (), s32[]{:S(2)}) async-start(), calls=%async_computation.14 | async-start | bytes 3276800 | tf_op jit(solution)/shard_map/reduce_scatter | solution.py:122
  282.2 30.3 %all-to-all-start.7 = ((bf16[20,8,2048]{2,0,1:T(8,128)(2,1)}), bf16[20,8,2048]{2,0,1:T(8,128)(2,1)S(1)}, u32[]{:S(2)}, u32[]{:S(2)}) async-start(bf16[20,8,2048]{2,0,1:T(8,128)(2,1)} %copy.91), calls=%async_computation.9 | async-start | bytes 1572864 | tf_op jit(solution)/shard_map/all_to_all | solution.py:124
Sparse Core Ops, SparseCore 0:
  9.2 29.3 all-gather.3
  40.4 65.1 all-gather.5
  136.5 40.9 all-gather.7
  226.9 12.9 reduce-scatter.2
  242.5 37.3 reduce-scatter.4

commit v4 on v3

--- a/solution.py
+++ b/solution.py
@@ -38,11 +38,11 @@
 
 
 def dispatch(blocks):
-    arrived = lax.all_to_all(blocks, "ez", split_axis=1, concat_axis=1, tiled=True)
     n_ey = lax.axis_size("ey")
-    copies = jnp.broadcast_to(arrived[None], (n_ey,) + arrived.shape)
-    across = lax.all_to_all(copies, "ey", split_axis=0, concat_axis=0, tiled=True)
-    pair = jnp.broadcast_to(across[None], (CORES,) + across.shape)
+    copies = jnp.broadcast_to(blocks[:, :, None], blocks.shape[:2] + (n_ey,) + blocks.shape[2:])
+    copies = copies.reshape(blocks.shape[0], -1, blocks.shape[2])
+    arrived = lax.all_to_all(copies, ("ez", "ey"), split_axis=1, concat_axis=1, tiled=True)
+    pair = jnp.broadcast_to(arrived[None], (CORES,) + arrived.shape)
     return lax.all_to_all(pair, "ec", split_axis=0, concat_axis=0, tiled=True)
 
 
@@ -83,8 +83,8 @@
     mapped = jnp.dot(
         incoming.reshape(-1, att_dim), att_matrix, preferred_element_type=jnp.float32
     ).astype(jnp.bfloat16)
-    mapped = mapped.reshape(CORES, n_ey, capacity, n_ez, out_slice)
-    mapped = jnp.transpose(mapped, (3, 1, 0, 2, 4)).reshape(
+    mapped = mapped.reshape(CORES, capacity, n_ez, n_ey, out_slice)
+    mapped = jnp.transpose(mapped, (2, 3, 0, 1, 4)).reshape(
         n_ez * n_ey * CORES, capacity, out_slice
     )
     back = lax.all_to_all(mapped, ("ez", "ey", "ec"), split_axis=0, concat_axis=0, tiled=True)
@@ -116,13 +116,12 @@
     projected = jnp.dot(
         activated, down_matrix, preferred_element_type=jnp.float32
     ).astype(jnp.bfloat16)
-    projected = projected.reshape(CORES, n_ey * capacity * n_ez, model_width)
+    projected = projected.reshape(CORES, capacity * n_ez * n_ey, model_width)
     reduced = lax.psum_scatter(projected, "ec", scatter_dimension=0, tiled=True)[0]
-    reduced = reduced.reshape(n_ey, capacity * n_ez, model_width)
-    reduced = lax.psum_scatter(reduced, "ey", scatter_dimension=0, tiled=True)[0]
-    reduced = reduced.reshape(capacity, n_ez, model_width)
-    summed = lax.all_to_all(reduced, "ez", split_axis=1, concat_axis=1, tiled=True)
-    summed = summed.reshape(capacity * EXPERTS, model_width).astype(jnp.float32)
+    reduced = reduced.reshape(capacity, n_ez * n_ey, model_width)
+    parts = lax.all_to_all(reduced, ("ez", "ey"), split_axis=1, concat_axis=1, tiled=True)
+    parts = parts.reshape(capacity, EXPERTS, n_ey, model_width).astype(jnp.float32)
+    summed = jnp.sum(parts, axis=2).reshape(capacity * EXPERTS, model_width)
     ffn_weight = pair_weights(ffn_logits, ffn_routes)
     weighted = ffn_place.astype(jnp.float32) * ffn_weight.reshape(1, -1)
     expert_mix = jnp.dot(weighted.T, summed, precision=lax.Precision.HIGHEST).reshape(

time: 322 us -> 386 us (1.20)
  waiting for transfers between devices: 128 us -> 261 us
  blocking collectives: 108 us -> 0 us
  starting transfers between devices: 25.6 us -> 51.3 us
  local copies, waits for them, and re-layouts: 14.2 us -> 24.9 us
    all_to_all x2 -> x3, waiting for transfers between devices: 46.3 us -> 211 us  [the longest x2 139 us: dispatch(): lax.all_to_all(copies, ('ez', 'ey'), split_axis=1, concat_axis=1, tiled=T...]
    all_to_all x4 -> x0, blocking collectives: 108 us -> none  [the longest x2 66.5 us: dispatch(): lax.all_to_all(copies, 'ey', split_axis=0, concat_axis=0, tiled=True)]
    reduce_scatter x1 -> x0, waiting for transfers between devices: 39.9 us -> none  [local(): lax.psum_scatter(reduced, 'ey', scatter_dimension=0, tiled=True)[0]]
    all_to_all x2 -> x3, starting transfers between devices: 10.7 us -> 26.7 us  [the longest x2 16.9 us: dispatch(): lax.all_to_all(copies, ('ez', 'ey'), split_axis=1, concat_axis=1, tiled=T...]
    all_to_all x1 -> x2, starting transfers between devices: 9.95 us -> 17.4 us  [dispatch(): return lax.all_to_all(pair, 'ec', split_axis=0, concat_axis=0, tiled=True)]
    broadcast_in_dim x4 -> x6, local copies, waits for them, and re-layouts: 4.27 us -> 10.7 us  [the longest x2 5.88 us: dispatch(): pair = jnp.broadcast_to(arrived[None], (CORES,) + arrived.shape)]
    all_to_all x1 -> x2, waiting for transfers between devices: 4.88 us -> 9.75 us  [dispatch(): return lax.all_to_all(pair, 'ec', split_axis=0, concat_axis=0, tiled=True)]
  transfers between devices with their start and end apart: 9 -> 10, of which waited for: 6 -> 7; matrix products, arithmetic and copies ran while one was open for 10% -> 10% of each run, Pallas kernels for 0% -> 0%
where the time goes in v4:
time: 386 us; the launch traced here: 384 us
  waiting for transfers between devices  261 us (68%)
  starting transfers between devices  51.3 us (13%)
  matrix products  30.7 us (8%)
  local copies, waits for them, and re-layouts  24.9 us (6%)
  between operations  13.5 us (3%)
    all_to_all x2, waiting for transfers between devices, dispatch(): lax.all_to_all(copies, ('ez', 'ey'), split_axis=1, concat_axis=1, tiled=T...  139 us
    all_to_all x1, waiting for transfers between devices, local(): lax.all_to_all(reduced, ('ez', 'ey'), split_axis=1, concat_axis=1, tiled=...  71.3 us
    all_to_all x1, waiting for transfers between devices, local(): lax.all_to_all(mapped, ('ez', 'ey', 'ec'), split_axis=0, concat_axis=0, t...  21.5 us
    all_to_all x2, starting transfers between devices, dispatch(): return lax.all_to_all(pair, 'ec', split_axis=0, concat_axis=0, tiled=True)  17.4 us
    all_to_all x2, starting transfers between devices, dispatch(): lax.all_to_all(copies, ('ez', 'ey'), split_axis=1, concat_axis=1, tiled=T...  16.9 us
    reduce_scatter x1, waiting for transfers between devices, local(): lax.psum_scatter(projected, 'ec', scatter_dimension=0, tiled=True)[0]  16.8 us
    dot_general x1, matrix products, local(): jnp.dot(flattened, gate_matrix.reshape(depth, 2 * hid_slice), preferred_e...  13.1 us
    dot_general x1, matrix products, local(): jnp.dot(activated, down_matrix, preferred_element_type=jnp.float32)  10.6 us
  transfers between devices with their start and end apart: 10, of which 7 were waited for; matrix products, arithmetic and copies ran while one was open for 10% of the time, Pallas kernels for 0%

profile of v4, /device:TPU:1, one launch (start us, length us, event | category | flops | bytes accessed | tf_op | source)
XLA Modules:
  0.0 384.2 jit_solution(12399376572787845042)
XLA Ops:
  10.6 2.0 broadcast_in_dim.33
  12.6 12.0 %all-to-all-start = ((bf16[20,32,2048]{2,0,1:T(8,128)(2,1)}), bf16[20,32,2048]{2,0,1:T(8,128)(2,1)S(1)}, u32[]{:S(2)}, u32[]{:S(2)}) async-start(bf16[20,32,2048]{2,0,1:T(8,128)(2,1)} %bitcast.82), calls=%async_computation | async-start | bytes 6291456 | tf_op jit(solution)/shard_map/all_to_all | solution.py:44
  25.4 69.6 %all-to-all-done = bf16[20,32,2048]{2,0,1:T(8,128)(2,1)S(1)} async-done(((bf16[20,32,2048]{2,0,1:T(8,128)(2,1)}), bf16[20,32,2048]{2,0,1:T(8,128)(2,1)S(1)}, u32[]{:S(2)}, u32[]{:S(2)}) %all-to-all-start) | async-done | bytes 2621472 | tf_op jit(solution)/shard_map/all_to_all | solution.py:44
  95.0 1.4 copy.115
  96.4 2.9 broadcast_in_dim.34
  99.4 8.8 %all-to-all-start.1 = ((bf16[2,20,32,2048]{3,2,1,0:T(8,128)(2,1)}), bf16[2,20,32,2048]{3,2,1,0:T(8,128)(2,1)}, u32[]{:S(2)}, u32[]{:S(2)}) async-start(bf16[2,20,32,2048]{3,2,1,0:T(8,128)(2,1)} %broadcast_in_dim.34), calls=%async_computation.1 | async-start | bytes 10485760 | tf_op jit(solution)/shard_map/all_to_all | solution.py:46
  108.2 4.9 %all-to-all-done.1 = bf16[2,20,32,2048]{3,2,1,0:T(8,128)(2,1)} async-done(((bf16[2,20,32,2048]{3,2,1,0:T(8,128)(2,1)}), bf16[2,20,32,2048]{3,2,1,0:T(8,128)(2,1)}, u32[]{:S(2)}, u32[]{:S(2)}) %all-to-all-start.1) | async-done | bytes 5242912 | tf_op jit(solution)/shard_map/all_to_all | solution.py:46
  113.1 4.3 %convolution_convert_fusion.1 = bf16[1280,256]{1,0:T(8,128)(2,1)S(1)} fusion(bf16[1280,2048]{1,0:T(8,128)(2,1)} %bitcast.3, bf16[1,2048,256]{2,1,0:T(8,128)(2,1)} %all-gather.4.cloned.1.call-done), kind=kOutput, calls=%fused_computation.7 | convolution fusion | flops 1342504960 | bytes 6946816 | tf_op jit(solution)/shard_map/dot_general | solution.py:83
  120.0 7.0 %all-to-all-start.2 = ((bf16[64,20,256]{2,1,0:T(8,128)(2,1)}), bf16[64,20,256]{2,1,0:T(8,128)(2,1)S(1)}, u32[]{:S(2)}, u32[]{:S(2)}) async-start(bf16[64,20,256]{2,1,0:T(8,128)(2,1)} %bitcast.6), calls=%async_computation.2 | async-start | bytes 1572864 | tf_op jit(solution)/shard_map/all_to_all | solution.py:90
  128.2 21.5 %all-to-all-done.2 = bf16[64,20,256]{2,1,0:T(8,128)(2,1)S(1)} async-done(((bf16[64,20,256]{2,1,0:T(8,128)(2,1)}), bf16[64,20,256]{2,1,0:T(8,128)(2,1)S(1)}, u32[]{:S(2)}, u32[]{:S(2)}) %all-to-all-start.2) | async-done | bytes 655392 | tf_op jit(solution)/shard_map/all_to_all | solution.py:90
  152.4 2.0 broadcast_in_dim.37
  154.4 4.9 %all-to-all-start.3 = ((bf16[20,32,2048]{2,0,1:T(8,128)(2,1)}), bf16[20,32,2048]{2,0,1:T(8,128)(2,1)S(1)}, u32[]{:S(2)}, u32[]{:S(2)}) async-start(bf16[20,32,2048]{2,0,1:T(8,128)(2,1)} %bitcast.83), calls=%async_computation.3 | async-start | bytes 6291456 | tf_op jit(solution)/shard_map/all_to_all | solution.py:44
  160.1 69.9 %all-to-all-done.3 = bf16[20,32,2048]{2,0,1:T(8,128)(2,1)S(1)} async-done(((bf16[20,32,2048]{2,0,1:T(8,128)(2,1)}), bf16[20,32,2048]{2,0,1:T(8,128)(2,1)S(1)}, u32[]{:S(2)}, u32[]{:S(2)}) %all-to-all-start.3) | async-done | bytes 2621472 | tf_op jit(solution)/shard_map/all_to_all | solution.py:44
  229.9 1.4 copy.123
  231.3 3.0 broadcast_in_dim.68
  234.3 8.6 %all-to-all-start.4 = ((bf16[2,20,32,2048]{3,2,1,0:T(8,128)(2,1)}), bf16[2,20,32,2048]{3,2,1,0:T(8,128)(2,1)}, u32[]{:S(2)}, u32[]{:S(2)}) async-start(bf16[2,20,32,2048]{3,2,1,0:T(8,128)(2,1)} %broadcast_in_dim.68), calls=%async_computation.4 | async-start | bytes 10485760 | tf_op jit(solution)/shard_map/all_to_all | solution.py:46
  242.9 4.9 %all-to-all-done.4 = bf16[2,20,32,2048]{3,2,1,0:T(8,128)(2,1)} async-done(((bf16[2,20,32,2048]{3,2,1,0:T(8,128)(2,1)}), bf16[2,20,32,2048]{3,2,1,0:T(8,128)(2,1)}, u32[]{:S(2)}, u32[]{:S(2)}) %all-to-all-start.4) | async-done | bytes 5242912 | tf_op jit(solution)/shard_map/all_to_all | solution.py:46
  247.7 13.1 %fusion = f32[1280,2,704]{0,2,1:T(8,128)} fusion(bf16[1280,2048,1]{1,0,2:T(8,128)(2,1)} %bitcast.16, bf16[1,2048,2,704]{1,3,2,0:T(8,128)(2,1)} %all-gather.6.cloned.1.call-done), kind=kOutput, calls=%fused_computation.2 | convolution fusion | flops 7381975040 | bytes 18219008 | tf_op jit(solution)/shard_map/dot_general | solution.py:111
  260.8 10.6 %convolution_convert_fusion = bf16[1280,2048]{1,0:T(8,128)(2,1)} fusion(bf16[1,704,2048]{2,1,0:T(8,128)(2,1)} %all-gather.8.cloned.1.call-done, f32[1280,2,704]{0,2,1:T(8,128)} %fusion), kind=kOutput, calls=%fused_computation | convolution fusion | flops 3699015680 | bytes 15335424 | tf_op jit(solution)/shard_map/dot_general | solution.py:116
  271.4 16.8 %reduce-scatter.2.cloned.1.call-done = bf16[1,640,2048]{2,1,0:T(8,128)(2,1)} async-done(((bf16[2,640,2048]{2,1,0:T(8,128)(2,1)}), bf16[1,640,2048]{2,1,0:T(8,128)(2,1)}) %reduce-scatter.2.cloned.1.call-update) | async-done | bytes 2621456 | tf_op jit(solution)/shard_map/reduce_scatter | solution.py:120
  288.2 4.9 %copy.124 = bf16[20,32,2048]{2,0,1:T(8,128)(2,1)} copy(bf16[20,32,2048]{2,1,0:T(8,128)(2,1)} %bitcast.85) | data formatting | bytes 5242880 | tf_op jit(solution)/shard_map/reshape;squeeze | solution.py:121
  293.1 9.8 %all-to-all-start.5 = ((bf16[20,32,2048]{2,0,1:T(8,128)(2,1)}), bf16[20,32,2048]{2,0,1:T(8,128)(2,1)S(1)}, u32[]{:S(2)}, u32[]{:S(2)}) async-start(bf16[20,32,2048]{2,0,1:T(8,128)(2,1)} %copy.124), calls=%async_computation.6 | async-start | bytes 6291456 | tf_op jit(solution)/shard_map/all_to_all | solution.py:122
  302.9 71.3 %all-to-all-done.5 = bf16[20,32,2048]{2,0,1:T(8,128)(2,1)S(1)} async-done(((bf16[20,32,2048]{2,0,1:T(8,128)(2,1)}), bf16[20,32,2048]{2,0,1:T(8,128)(2,1)S(1)}, u32[]{:S(2)}, u32[]{:S(2)}) %all-to-all-start.5) | async-done | bytes 2621472 | tf_op jit(solution)/shard_map/all_to_all | solution.py:122
  374.8 1.7 fusion.8
  (71 shorter events, 13.5 us)
Async XLA Ops:
  6.5 101.7 %all-gather.4.cloned.1.call-start = ((), (), s32[]{:S(2)}) async-start(), calls=%async_computation.7 | async-start | bytes 1310720 | tf_op jit(solution)/shard_map/all_gather | solution.py:71
  12.6 82.4 %all-to-all-start = ((bf16[20,32,2048]{2,0,1:T(8,128)(2,1)}), bf16[20,32,2048]{2,0,1:T(8,128)(2,1)S(1)}, u32[]{:S(2)}, u32[]{:S(2)}) async-start(bf16[20,32,2048]{2,0,1:T(8,128)(2,1)} %bitcast.82), calls=%async_computation | async-start | bytes 6291456 | tf_op jit(solution)/shard_map/all_to_all | solution.py:44
  24.7 218.2 %all-gather.6.cloned.1.call-start = ((), (), s32[]{:S(2)}) async-start(), calls=%async_computation.8 | async-start | bytes 7208960 | tf_op jit(solution)/shard_map/all_gather | solution.py:72
  99.4 13.7 %all-to-all-start.1 = ((bf16[2,20,32,2048]{3,2,1,0:T(8,128)(2,1)}), bf16[2,20,32,2048]{3,2,1,0:T(8,128)(2,1)}, u32[]{:S(2)}, u32[]{:S(2)}) async-start(bf16[2,20,32,2048]{3,2,1,0:T(8,128)(2,1)} %broadcast_in_dim.34), calls=%async_computation.1 | async-start | bytes 10485760 | tf_op jit(solution)/shard_map/all_to_all | solution.py:46
  117.4 9.8 %copy-start.3 = (s32[64,2]{0,1:T(2,128)S(1)}, s32[64,2]{0,1:T(2,128)}, u32[]{:S(2)}) copy-start(s32[64,2]{0,1:T(2,128)} %param.15) | copy-start | bytes 1540
  117.4 10.7 %copy-start.4 = (bf16[2048]{0:T(1024)(128)(2,1)S(1)}, bf16[2048]{0:T(1024)(128)(2,1)}, u32[]{:S(2)}) copy-start(bf16[2048]{0:T(1024)(128)(2,1)} %param.20) | copy-start | bytes 12292
  117.4 10.7 %copy-start.6 = (f32[64,8]{0,1:T(8,128)S(1)}, f32[64,8]{0,1:T(8,128)}, u32[]{:S(2)}) copy-start(f32[64,8]{0,1:T(8,128)} %param.14) | copy-start | bytes 6148
  117.4 10.7 %copy-start.8 = (s32[64,2]{0,1:T(2,128)S(1)}, s32[64,2]{0,1:T(2,128)}, u32[]{:S(2)}) copy-start(s32[64,2]{0,1:T(2,128)} %param.13) | copy-start | bytes 1540
  120.0 30.5 %copy-start.2 = (bf16[64,2048]{1,0:T(8,128)(2,1)S(1)}, bf16[64,2048]{1,0:T(8,128)(2,1)}, u32[]{:S(2)}) copy-start(bf16[64,2048]{1,0:T(8,128)(2,1)} %param.11) | copy-start | bytes 786436
  120.0 29.7 %all-to-all-start.2 = ((bf16[64,20,256]{2,1,0:T(8,128)(2,1)}), bf16[64,20,256]{2,1,0:T(8,128)(2,1)S(1)}, u32[]{:S(2)}, u32[]{:S(2)}) async-start(bf16[64,20,256]{2,1,0:T(8,128)(2,1)} %bitcast.6), calls=%async_computation.2 | async-start | bytes 1572864 | tf_op jit(solution)/shard_map/all_to_all | solution.py:90
  150.8 0.8 copy-start
  154.4 75.5 %all-to-all-start.3 = ((bf16[20,32,2048]{2,0,1:T(8,128)(2,1)}), bf16[20,32,2048]{2,0,1:T(8,128)(2,1)S(1)}, u32[]{:S(2)}, u32[]{:S(2)}) async-start(bf16[20,32,2048]{2,0,1:T(8,128)(2,1)} %bitcast.83), calls=%async_computation.3 | async-start | bytes 6291456 | tf_op jit(solution)/shard_map/all_to_all | solution.py:44
  159.3 101.5 %all-gather.8.cloned.1.call-start = ((), (), s32[]{:S(2)}) async-start(), calls=%async_computation.9 | async-start | bytes 3604480 | tf_op jit(solution)/shard_map/all_gather | solution.py:73
  234.3 13.4 %all-to-all-start.4 = ((bf16[2,20,32,2048]{3,2,1,0:T(8,128)(2,1)}), bf16[2,20,32,2048]{3,2,1,0:T(8,128)(2,1)}, u32[]{:S(2)}, u32[]{:S(2)}) async-start(bf16[2,20,32,2048]{3,2,1,0:T(8,128)(2,1)} %broadcast_in_dim.68), calls=%async_computation.4 | async-start | bytes 10485760 | tf_op jit(solution)/shard_map/all_to_all | solution.py:46
  242.9 45.4 %reduce-scatter.2.cloned.1.call-start = ((), (), s32[]{:S(2)}) async-start(), calls=%async_computation.10 | async-start | bytes 7864320 | tf_op jit(solution)/shard_map/reduce_scatter | solution.py:120
  293.1 9.8 %copy-start.5 = (bf16[2048]{0:T(1024)(128)(2,1)S(1)}, bf16[2048]{0:T(1024)(128)(2,1)}, u32[]{:S(2)}) copy-start(bf16[2048]{0:T(1024)(128)(2,1)} %param.21) | copy-start | bytes 12292
  293.1 9.8 %copy-start.7 = (f32[64,8]{0,1:T(8,128)S(1)}, f32[64,8]{0,1:T(8,128)}, u32[]{:S(2)}) copy-start(f32[64,8]{0,1:T(8,128)} %param.16) | copy-start | bytes 6148
  293.1 81.2 %all-to-all-start.5 = ((bf16[20,32,2048]{2,0,1:T(8,128)(2,1)}), bf16[20,32,2048]{2,0,1:T(8,128)(2,1)S(1)}, u32[]{:S(2)}, u32[]{:S(2)}) async-start(bf16[20,32,2048]{2,0,1:T(8,128)(2,1)} %copy.124), calls=%async_computation.6 | async-start | bytes 6291456 | tf_op jit(solution)/shard_map/all_to_all | solution.py:122
  374.2 2.3 copy-start.1
Sparse Core Ops, SparseCore 0:
  9.2 29.3 all-gather.3
  40.4 65.0 all-gather.5
  162.0 41.6 all-gather.7
  271.6 16.6 reduce-scatter.1
